TPU v7x, 512 devices: a whole 4x8x8 slice. The times are simulated.
512 devices in a mesh: fsdp: 128 (over z, x_lo, y), dp: 4 (over x_hi, core).
Axes of the slice: x: 4 (x_hi: 2, x_lo: 2; x = x_hi * 2 + x_lo), y: 8, z: 8, core: 2. Of those that a mesh axis runs over, the one named last changes fastest.
Arguments:
- glu_input: bfloat16 [131072, 3072], P(('fsdp', 'dp')), may hold values from -6 to 6
- frame_counts: int32 [512, 8], P(('fsdp', 'dp')), may hold values from 1 to 128, as said below
- send_rows: int32 [512, 256], P(('fsdp', 'dp')), may hold values from 0 to 256, as said below
- owner_rows: int32 [512, 160], P(('fsdp', 'dp')), may hold values from 0 to 255, as said below
- depth_kernel: float32 [5, 1536], replicated, may hold values from -2.5 to 2.5
- norm_gain: float32 [1536], replicated, may hold values from 0.25 to 1.75
- norm_bias: float32 [1536], replicated, may hold values from -3 to 3
- point_weight: bfloat16 [1536, 1536], P('fsdp'), may hold values from -0.15625 to 0.15625
- cotangent: bfloat16 [81920, 1536], P(('fsdp', 'dp')), may hold values from -6 to 6
Outputs:
- output: bfloat16 [81920, 1536], P(('fsdp', 'dp'))
- input_grad: bfloat16 [131072, 3072], P(('fsdp', 'dp'))
- kernel_grad: float32 [5, 1536], replicated
- norm_grad: float32 [2, 1536], replicated
Inputs may be any that keep to these rules, and one draw needn't show every extreme that they name: `frame_counts`: A device's counts are the lengths of its 8 utterances. A device's total lies from 64 to 256, both reached at every dp index, and the totals of the devices with one dp index sum to 160 times the fsdp axis size. The longest utterance is reached at every dp index. `send_rows`: entry q of a device's list names the local slot whose activation goes to fsdp index q // 2 with the same dp index, as that owner's position q % 2 from this device; the value 256 marks an unused entry. Each live slot is named once, positions for one owner are used from the lowest up, and some device of every dp index fills all 2 positions for every owner. `owner_rows`: entry b names received position p: position p % 2 from fsdp index p // 2 of the same dp index. The 160 entries are distinct and are exactly the positions that senders use for this owner.
All inputs are finite; a program needn't handle non-finite values.
Results may differ from a plain program's by a relative error of at most 0.0085.
Values may be sent and summed in bfloat16 or wider, within the bound.
No kernel may reach another device: no remote copies, remote signals or barrier semaphores. Data moves between devices by JAX's collectives and lax.ppermute only.
A program may use at most 64 MiB of HBM per device.

v0:
```python
import math

import jax
import jax.numpy as jnp
from jax import lax
from jax.sharding import PartitionSpec as P

eps = 1e-05


def conv_module(glu_rows, counts, kernel, gain_vec, bias_vec):
    row_count = glu_rows.shape[0]
    chan_count = kernel.shape[1]
    half_width = kernel.shape[0] // 2
    values = glu_rows.astype(jnp.float32)
    mixed_vals = values[:, :chan_count] * jax.nn.sigmoid(values[:, chan_count:])
    utter_ends = jnp.cumsum(counts)
    position = jnp.arange(row_count, dtype=jnp.int32)
    segment = jnp.sum((position[:, None] >= utter_ends[None, :]).astype(jnp.int32), axis=1)
    is_live = position < utter_ends[-1]
    mixed_vals = jnp.where(is_live[:, None], mixed_vals, 0.0)
    padded = jnp.pad(mixed_vals, ((half_width, half_width), (0, 0)))
    labels = jnp.pad(segment, (half_width, half_width), constant_values=-1)
    conv_out = jnp.zeros((row_count, chan_count), jnp.float32)
    for offset in range(2 * half_width + 1):
        same_utt = labels[offset : offset + row_count] == segment
        conv_out = (
            conv_out
            + jnp.where(same_utt[:, None], padded[offset : offset + row_count], 0.0)
            * kernel[offset]
        )
    center = jnp.mean(conv_out, axis=1, keepdims=True)
    spread = jnp.mean(jnp.square(conv_out - center), axis=1, keepdims=True)
    normed = (conv_out - center) * lax.rsqrt(spread + eps) * gain_vec + bias_vec
    activated = normed * jax.nn.sigmoid(normed)
    return jnp.where(is_live[:, None], activated, 0.0)


def per_device(
    glu_input,
    frame_counts,
    send_rows,
    owner_rows,
    depth_kernel,
    norm_gain,
    norm_bias,
    point_weight,
    cotangent,
):
    counts = frame_counts[0]
    send_slot = send_rows[0]
    owner_slot = owner_rows[0]
    row_count = glu_input.shape[0]
    out_count = point_weight.shape[1]

    def local_pass(glu_rows, kernel, gain_vec, bias_vec):
        return conv_module(glu_rows, counts, kernel, gain_vec, bias_vec)

    activated, pullback = jax.vjp(local_pass, glu_input, depth_kernel, norm_gain, norm_bias)
    activations = activated.astype(jnp.bfloat16)
    produced = jnp.dot(
        activations,
        lax.all_gather(point_weight, "fsdp", axis=0, tiled=True),
        preferred_element_type=jnp.float32,
    ).astype(jnp.bfloat16)
    outgoing = jnp.concatenate([produced, jnp.zeros((1, out_count), jnp.bfloat16)], axis=0)[
        send_slot
    ]
    arrived = lax.all_to_all(outgoing, "fsdp", split_axis=0, concat_axis=0, tiled=True)
    output = arrived[owner_slot]
    parked = jnp.zeros((row_count, out_count), jnp.bfloat16).at[owner_slot].set(cotangent)
    returned = lax.all_to_all(parked, "fsdp", split_axis=0, concat_axis=0, tiled=True)
    home_rows = (
        jnp.zeros((row_count + 1, out_count), jnp.bfloat16).at[send_slot].set(returned)[:row_count]
    )
    grad_acts = lax.dot_general(
        home_rows,
        lax.all_gather(point_weight, "fsdp", axis=0, tiled=True),
        (((1,), (1,)), ((), ())),
        preferred_element_type=jnp.float32,
    ).astype(jnp.bfloat16)
    input_grad, kernel_part, gain_part, bias_part = pullback(grad_acts.astype(jnp.float32))
    totals = lax.psum((kernel_part, jnp.stack([gain_part, bias_part])), ("fsdp", "dp"))
    frame_total = owner_slot.shape[0] * lax.axis_size("fsdp") * lax.axis_size("dp")
    grad_scale = 1.0 / math.sqrt(frame_total)
    return (output, input_grad, totals[0] * grad_scale, totals[1] * grad_scale)


def solution(mesh):
    in_specs = (
        P(("fsdp", "dp"), None),
        P(("fsdp", "dp"), None),
        P(("fsdp", "dp"), None),
        P(("fsdp", "dp"), None),
        P(),
        P(),
        P(),
        P("fsdp", None),
        P(("fsdp", "dp"), None),
    )
    out_specs = (P(("fsdp", "dp"), None), P(("fsdp", "dp"), None), P(), P())
    return jax.shard_map(
        per_device, mesh=mesh, in_specs=in_specs, out_specs=out_specs, check_vma=False
    )
```

profile of v0, /device:TPU:1, one launch (start us, length us, event | category | flops | bytes accessed | tf_op | source)
XLA Modules:
  0.0 759.5 jit_solution(14914906572277938264)
XLA Ops:
  7.9 0.7 compare_select_fusion
  8.6 2.1 scatter_custom_fusion
  10.7 1.2 all_to_all.19
  11.9 19.4 %all-to-all-start.1 = ((bf16[128,2,1536]{2,1,0:T(2,128)(2,1)}), bf16[128,2,1536]{2,1,0:T(2,128)(2,1)S(1)}, u32[]{:S(2)}, u32[]{:S(2)}) async-start(bf16[128,2,1536]{2,1,0:T(2,128)(2,1)} %all_to_all.19), calls=%async_computation.1 | async-start | bytes 1572864 | tf_op jit(solution)/shard_map/all_to_all | solution.py:72
  33.9 1.3 copy-done
  35.2 1.7 fusion.30
  37.2 21.3 %all-to-all-done.1 = bf16[128,2,1536]{2,1,0:T(2,128)(2,1)S(1)} async-done(((bf16[128,2,1536]{2,1,0:T(2,128)(2,1)}), bf16[128,2,1536]{2,1,0:T(2,128)(2,1)S(1)}, u32[]{:S(2)}, u32[]{:S(2)}) %all-to-all-start.1) | async-done | bytes 786464 | tf_op jit(solution)/shard_map/all_to_all | solution.py:72
  58.8 2.7 scatter_custom_fusion.1
  61.5 458.1 %all-gather.3.cloned.1.call-done = bf16[128,12,1536]{2,1,0:T(8,128)(2,1)} async-done(((bf16[1,12,1536]{2,1,0:T(8,128)(2,1)}), bf16[128,12,1536]{2,1,0:T(8,128)(2,1)}) %all-gather.3.cloned.1.call-update) | async-done | bytes 4718608 | tf_op jit(solution)/shard_map/all_gather | solution.py:63
  519.6 8.2 %reshape.190 = bf16[1536,1536]{1,0:T(8,128)(2,1)} reshape(bf16[128,12,1536]{2,1,0:T(8,128)(2,1)} %all-gather.3.cloned.1.call-done) | data formatting | bytes 9437184
  527.9 3.9 convolution_convert_fusion.1
  531.8 1.3 gather_fusion
  533.1 1.2 all_to_all.16
  534.3 7.4 all-to-all-start
  541.8 4.6 multiply_reduce_fusion
  546.7 1.1 copy-done.3
  547.8 2.4 multiply_reduce_fusion.5
  550.2 0.8 multiply_select_fusion.3
  550.9 1.1 copy-done.1
  552.1 1.4 fusion.4
  554.0 192.0 %all-reduce.15 = (f32[5,1536]{1,0:T(8,128)S(1)}, f32[2,1536]{1,0:T(2,128)S(1)}) all-reduce(f32[5,1536]{1,0:T(8,128)S(1)} %pad_add_fusion.4, f32[2,1536]{1,0:T(2,128)S(1)} %pad_maximum_fusion), channel_id=1, replica_groups=mesh['fsdp'=128,'dp'=4] {'fsdp','dp'}, use_global_device_ids=true, to_apply=%region_14.15 | all-reduce | flops 10752 | bytes 86016 | tf_op jit(solution)/shard_map/psum | solution.py:83
  746.1 1.3 add_convert_fusion
  748.6 2.3 all_to_all.18
  750.9 1.8 gather_fusion.1
  (53 shorter events, 6.0 us)
Async XLA Ops:
  7.2 512.5 %all-gather.3.cloned.1.call-start = ((), (), s32[]{:S(2)}) async-start(), calls=%async_computation.2 | async-start | bytes 6340608 | tf_op jit(solution)/shard_map/all_gather | solution.py:63
  10.7 20.6 %copy-start.10 = (s32[1,8]{1,0:T(1,128)S(1)}, s32[1,8]{1,0:T(1,128)}, u32[]{:S(2)}) copy-start(s32[1,8]{1,0:T(1,128)} %param.10) | copy-start | bytes 100
  10.7 21.4 %copy-start.8 = (s32[1,256]{1,0:T(1,128)S(1)}, s32[1,256]{1,0:T(1,128)}, u32[]{:S(2)}) copy-start(s32[1,256]{1,0:T(1,128)} %param.11) | copy-start | bytes 3076
  10.7 21.5 %copy-start.6 = (f32[5,1536]{1,0:T(8,128)S(1)}, f32[5,1536]{1,0:T(8,128)}, u32[]{:S(2)}) copy-start(f32[5,1536]{1,0:T(8,128)} %param.13) | copy-start | bytes 92164
  11.9 21.1 %copy-start.4 = (bf16[256,3072]{1,0:T(8,128)(2,1)S(1)}, bf16[256,3072]{1,0:T(8,128)(2,1)}, u32[]{:S(2)}) copy-start(bf16[256,3072]{1,0:T(8,128)(2,1)} %param.9) | copy-start | bytes 4718596
  11.9 46.6 %all-to-all-start.1 = ((bf16[128,2,1536]{2,1,0:T(2,128)(2,1)}), bf16[128,2,1536]{2,1,0:T(2,128)(2,1)S(1)}, u32[]{:S(2)}, u32[]{:S(2)}) async-start(bf16[128,2,1536]{2,1,0:T(2,128)(2,1)} %all_to_all.19), calls=%async_computation.1 | async-start | bytes 1572864 | tf_op jit(solution)/shard_map/all_to_all | solution.py:72
  33.4 1.8 copy-start
  35.2 1.7 copy-start.2
  61.5 466.4 %copy-start.7 = (f32[1536]{0:T(1024)S(1)}, f32[1536]{0:T(1024)}, u32[]{:S(2)}) copy-start(f32[1536]{0:T(1024)} %param.14) | copy-start | bytes 18436
  61.5 466.4 %copy-start.9 = (f32[1536]{0:T(1024)S(1)}, f32[1536]{0:T(1024)}, u32[]{:S(2)}) copy-start(f32[1536]{0:T(1024)} %param.15) | copy-start | bytes 18436
  533.1 8.6 %copy-start.5 = (bf16[257,1536]{1,0:T(8,128)(2,1)S(1)}, bf16[257,1536]{1,0:T(8,128)(2,1)}, u32[]{:S(2)}) copy-start(bf16[257,1536]{1,0:T(8,128)(2,1)} %scatter_custom_fusion.1) | copy-start | bytes 2368516
  534.3 214.3 %all-to-all-start = ((bf16[128,2,1536]{2,1,0:T(2,128)(2,1)}), bf16[128,2,1536]{2,1,0:T(2,128)(2,1)}, u32[]{:S(2)}, u32[]{:S(2)}) async-start(bf16[128,2,1536]{2,1,0:T(2,128)(2,1)} %all_to_all.16), calls=%async_computation | async-start | bytes 1572864 | tf_op jit(solution)/shard_map/all_to_all | solution.py:69
  546.4 1.4 copy-start.3
  550.2 1.9 copy-start.1
Sparse Core Ops, SparseCore 0:
  10.1 509.5 all-gather.2
where the time goes:
time: 760 us
  waiting for transfers between devices  480 us (63%)
  blocking collectives  192 us (25%)
  starting transfers between devices  26.9 us (4%)
  local copies, waits for them, and re-layouts  25.3 us (3%)
  between operations  14.4 us (2%)
  other arithmetic  12.3 us (2%)
  matrix products  8.52 us (1%)
    all_gather x1, waiting for transfers between devices, per_device(): lax.all_gather(point_weight, 'fsdp', axis=0, tiled=True)  458 us
    psum x1, blocking collectives, per_device(): lax.psum((kernel_part, jnp.stack([gain_part, bias_part])), ('fsdp', 'dp'))  192 us
    all_to_all x1, waiting for transfers between devices, per_device(): lax.all_to_all(parked, 'fsdp', split_axis=0, concat_axis=0, tiled=True)  21.3 us
    all_to_all x1, starting transfers between devices, per_device(): lax.all_to_all(parked, 'fsdp', split_axis=0, concat_axis=0, tiled=True)  19.4 us
  transfers between devices with their start and end apart: 3, of which 2 were waited for; matrix products, arithmetic and copies ran while one was open for 3% of the time, Pallas kernels for 0%

commit v1 on v0

--- a/solution.py
+++ b/solution.py
@@ -3,9 +3,25 @@
 import jax
 import jax.numpy as jnp
 from jax import lax
-from jax.sharding import PartitionSpec as P
+from jax.sharding import Mesh, PartitionSpec as P
 
 eps = 1e-05
+
+FSDP = ("z", "xl", "y")
+DP = ("xh", "c")
+ALL = FSDP + DP
+
+
+def gather_weight(w):
+    w = lax.all_gather(w, "y", axis=0, tiled=True)
+    w = lax.all_gather(w, "xl", axis=0, tiled=True)
+    return lax.all_gather(w, "z", axis=0, tiled=True)
+
+
+def sum_all(tree):
+    for axis in ("c", "xh", "xl", "y", "z"):
+        tree = lax.psum(tree, axis)
+    return tree
 
 
 def conv_module(glu_rows, counts, kernel, gain_vec, bias_vec):
@@ -58,47 +74,54 @@
 
     activated, pullback = jax.vjp(local_pass, glu_input, depth_kernel, norm_gain, norm_bias)
     activations = activated.astype(jnp.bfloat16)
+    full_weight = gather_weight(point_weight)
     produced = jnp.dot(
         activations,
-        lax.all_gather(point_weight, "fsdp", axis=0, tiled=True),
+        full_weight,
         preferred_element_type=jnp.float32,
     ).astype(jnp.bfloat16)
     outgoing = jnp.concatenate([produced, jnp.zeros((1, out_count), jnp.bfloat16)], axis=0)[
         send_slot
     ]
-    arrived = lax.all_to_all(outgoing, "fsdp", split_axis=0, concat_axis=0, tiled=True)
+    arrived = lax.all_to_all(outgoing, FSDP, split_axis=0, concat_axis=0, tiled=True)
     output = arrived[owner_slot]
     parked = jnp.zeros((row_count, out_count), jnp.bfloat16).at[owner_slot].set(cotangent)
-    returned = lax.all_to_all(parked, "fsdp", split_axis=0, concat_axis=0, tiled=True)
+    returned = lax.all_to_all(parked, FSDP, split_axis=0, concat_axis=0, tiled=True)
     home_rows = (
         jnp.zeros((row_count + 1, out_count), jnp.bfloat16).at[send_slot].set(returned)[:row_count]
     )
     grad_acts = lax.dot_general(
         home_rows,
-        lax.all_gather(point_weight, "fsdp", axis=0, tiled=True),
+        full_weight,
         (((1,), (1,)), ((), ())),
         preferred_element_type=jnp.float32,
     ).astype(jnp.bfloat16)
     input_grad, kernel_part, gain_part, bias_part = pullback(grad_acts.astype(jnp.float32))
-    totals = lax.psum((kernel_part, jnp.stack([gain_part, bias_part])), ("fsdp", "dp"))
-    frame_total = owner_slot.shape[0] * lax.axis_size("fsdp") * lax.axis_size("dp")
+    totals = sum_all((kernel_part, jnp.stack([gain_part, bias_part])))
+    frame_total = owner_slot.shape[0] * lax.axis_size(ALL)
     grad_scale = 1.0 / math.sqrt(frame_total)
     return (output, input_grad, totals[0] * grad_scale, totals[1] * grad_scale)
 
 
+def split_mesh(mesh):
+    n_fsdp, n_dp = mesh.shape["fsdp"], mesh.shape["dp"]
+    shape = (n_fsdp // 16, 2, 8, n_dp // 2, 2)
+    return Mesh(mesh.devices.reshape(shape), FSDP + DP)
+
+
 def solution(mesh):
     in_specs = (
-        P(("fsdp", "dp"), None),
-        P(("fsdp", "dp"), None),
-        P(("fsdp", "dp"), None),
-        P(("fsdp", "dp"), None),
+        P(ALL, None),
+        P(ALL, None),
+        P(ALL, None),
+        P(ALL, None),
         P(),
         P(),
         P(),
-        P("fsdp", None),
-        P(("fsdp", "dp"), None),
+        P(FSDP, None),
+        P(ALL, None),
     )
-    out_specs = (P(("fsdp", "dp"), None), P(("fsdp", "dp"), None), P(), P())
+    out_specs = (P(ALL, None), P(ALL, None), P(), P())
     return jax.shard_map(
-        per_device, mesh=mesh, in_specs=in_specs, out_specs=out_specs, check_vma=False
+        per_device, mesh=split_mesh(mesh), in_specs=in_specs, out_specs=out_specs, check_vma=False
     )

time: 760 us -> 248 us (0.33)
  the two profiles are of different devices: /device:TPU:1 before, /device:TPU:2 now
where the time goes in v1:
time: 248 us
  blocking collectives  121 us (49%)
  waiting for transfers between devices  50.5 us (20%)
  starting transfers between devices  24.8 us (10%)
  local copies, waits for them, and re-layouts  17.2 us (7%)
  between operations  14.4 us (6%)
  other arithmetic  11.6 us (5%)
  matrix products  8.63 us (3%)
    psum x5, blocking collectives, sum_all(): tree = lax.psum(tree, axis)  83.9 us
    all_gather x1, waiting for transfers between devices, gather_weight(): return lax.all_gather(w, 'z', axis=0, tiled=True)  38 us
    all_gather x1, blocking collectives, gather_weight(): w = lax.all_gather(w, 'y', axis=0, tiled=True)  26.8 us
    all_to_all x1, starting transfers between devices, per_device(): lax.all_to_all(parked, FSDP, split_axis=0, concat_axis=0, tiled=True)  14.4 us
    all_to_all x1, waiting for transfers between devices, per_device(): lax.all_to_all(parked, FSDP, split_axis=0, concat_axis=0, tiled=True)  12.4 us
    all_to_all x1, starting transfers between devices, per_device(): lax.all_to_all(outgoing, FSDP, split_axis=0, concat_axis=0, tiled=True)  10.3 us
    all_gather x1, blocking collectives, gather_weight(): w = lax.all_gather(w, 'xl', axis=0, tiled=True)  9.96 us
  transfers between devices with their start and end apart: 3, of which 2 were waited for; matrix products, arithmetic and copies ran while one was open for 9% of the time, Pallas kernels for 0%

profile of v1, /device:TPU:2, one launch (start us, length us, event | category | flops | bytes accessed | tf_op | source)
XLA Modules:
  0.0 247.8 jit_solution(17268215064795342908)
XLA Ops:
  7.2 26.8 %all-gather = bf16[8,12,1536]{2,1,0:T(8,128)(2,1)S(1)} all-gather(bf16[1,12,1536]{2,1,0:T(8,128)(2,1)} %bitcast.12), channel_id=1, replica_groups=mesh['z'=8,'xl'=2,'y'=8,'xh'=2,'c'=2] {'y'}, dimensions={0}, use_global_device_ids=true | all-gather | bytes 331776 | tf_op jit(solution)/shard_map/all_gather | solution.py:16
  34.1 10.0 %all_gather.10 = bf16[192,1536]{1,0:T(8,128)(2,1)} all-gather(bf16[96,1536]{1,0:T(8,128)(2,1)S(1)} %reshape.190), channel_id=1, replica_groups=mesh['z'=8,'xl'=2,'y'=8,'xh'=2,'c'=2] {'xl'}, dimensions={0}, use_global_device_ids=true | all-gather | bytes 884736 | tf_op jit(solution)/shard_map/all_gather | solution.py:17
  44.1 2.1 scatter_custom_fusion
  47.5 14.4 %all-to-all-start.1 = ((bf16[128,2,1536]{2,1,0:T(2,128)(2,1)}), bf16[128,2,1536]{2,1,0:T(2,128)(2,1)S(1)}, u32[]{:S(2)}, u32[]{:S(2)}) async-start(bf16[128,2,1536]{2,1,0:T(2,128)(2,1)} %all_to_all.19), calls=%async_computation.1 | async-start | bytes 1572864 | tf_op jit(solution)/shard_map/all_to_all | solution.py:89
  64.5 1.2 copy-done
  65.7 1.6 fusion.30
  67.7 12.4 %all-to-all-done.1 = bf16[128,2,1536]{2,1,0:T(2,128)(2,1)S(1)} async-done(((bf16[128,2,1536]{2,1,0:T(2,128)(2,1)}), bf16[128,2,1536]{2,1,0:T(2,128)(2,1)S(1)}, u32[]{:S(2)}, u32[]{:S(2)}) %all-to-all-start.1) | async-done | bytes 786464 | tf_op jit(solution)/shard_map/all_to_all | solution.py:89
  80.4 2.7 %scatter_custom_fusion.1 = bf16[257,1536]{1,0:T(8,128)(2,1)} fusion(s32[256]{0:T(256)S(1)} %bitcast.14, bf16[256,1536]{1,0:T(8,128)(2,1)S(1)} %reshape.185, bf16[]{:T(256)} %constant.43.clone.1), kind=kCustom, calls=%fused_computation.56 | custom fusion | bytes 789506 | tf_op jit(solution)/shard_map/scatter | solution.py:91
  83.1 38.0 %all-gather.3.cloned.1.call-done = bf16[1536,1536]{1,0:T(8,128)(2,1)} async-done(((bf16[192,1536]{1,0:T(8,128)(2,1)}), bf16[1536,1536]{1,0:T(8,128)(2,1)}) %all-gather.3.cloned.1.call-update) | async-done | bytes 4718608 | tf_op jit(solution)/shard_map/all_gather | solution.py:18
  121.1 3.9 %convolution_convert_fusion.1 = bf16[256,1536]{1,0:T(8,128)(2,1)S(1)} fusion(bf16[1536,1536]{1,0:T(8,128)(2,1)} %all-gather.3.cloned.1.call-done, f32[256,1536]{1,0:T(8,128)S(1)} %get-tuple-element.32, f32[1536]{0:T(1024)S(1)} %copy-done.10, f32[1536]{0:T(1024)S(1)} %copy-done.7, f32[256]{0:T(256)S(1)} %fusion.25, f32[256]{0:T(256)S(1)} %broadcast_multiply_fusion.3, ...), kind=kOutput, calls=%fused_computation.8 | convolution fusion | flops 1212284928 | bytes 7092480 | tf_op jit(solution)/shard_map/dot_general | solution.py:78
  125.1 1.3 gather_fusion
  126.4 1.3 all_to_all.16
  127.7 10.3 %all-to-all-start = ((bf16[128,2,1536]{2,1,0:T(2,128)(2,1)}), bf16[128,2,1536]{2,1,0:T(2,128)(2,1)}, u32[]{:S(2)}, u32[]{:S(2)}) async-start(bf16[128,2,1536]{2,1,0:T(2,128)(2,1)} %all_to_all.16), calls=%async_computation | async-start | bytes 1572864 | tf_op jit(solution)/shard_map/all_to_all | solution.py:86
  138.0 4.7 %multiply_reduce_fusion = (f32[1536]{0:T(1024)S(1)}, f32[256]{0:T(256)S(1)}, f32[256]{0:T(256)S(1)}, f32[1536]{0:T(1024)S(1)}, f32[256,1536]{1,0:T(8,128)S(1)}) fusion(f32[256,1536]{1,0:T(8,128)S(1)} %get-tuple-element.32, f32[256]{0:T(256)S(1)} %fusion.25, f32[256]{0:T(256)S(1)} %broadcast_multiply_fusion.3, f32[1536]{0:T(1024)S(1)} %copy-done.7, ...), kind=kOutput, calls=%fused_computation.23 | convolution fusion | flops 1217393152 | bytes 8684032 | tf_op jit(solution)/shard_map/dot_general | solution.py:93
  144.2 2.4 multiply_reduce_fusion.5
  148.4 1.4 fusion.4
  150.4 3.6 %all-reduce.17 = (f32[5,1536]{1,0:T(8,128)S(1)}, f32[2,1536]{1,0:T(2,128)S(1)}) all-reduce(f32[5,1536]{1,0:T(8,128)S(1)} %pad_add_fusion.4, f32[2,1536]{1,0:T(2,128)S(1)} %pad_maximum_fusion), channel_id=1, replica_groups=mesh['z'=8,'xl'=2,'y'=8,'xh'=2,'c'=2] {'c'}, use_global_device_ids=true, to_apply=%region_14.15 | all-reduce | flops 10752 | bytes 86016 | tf_op jit(solution)/shard_map/psum | solution.py:23
  154.0 11.0 %all-reduce.18 = (f32[5,1536]{1,0:T(8,128)S(1)}, f32[2,1536]{1,0:T(2,128)S(1)}) all-reduce(f32[5,1536]{1,0:T(8,128)S(1)} %get-tuple-element.22, f32[2,1536]{1,0:T(2,128)S(1)} %get-tuple-element.23), channel_id=1, replica_groups=mesh['z'=8,'xl'=2,'y'=8,'xh'=2,'c'=2] {'xh'}, use_global_device_ids=true, to_apply=%region_15.16 | all-reduce | flops 10752 | bytes 86016 | tf_op jit(solution)/shard_map/psum | solution.py:23
  165.0 8.8 %all-reduce.19 = (f32[5,1536]{1,0:T(8,128)S(1)}, f32[2,1536]{1,0:T(2,128)S(1)}) all-reduce(f32[5,1536]{1,0:T(8,128)S(1)} %get-tuple-element.24, f32[2,1536]{1,0:T(2,128)S(1)} %get-tuple-element.25), channel_id=1, replica_groups=mesh['z'=8,'xl'=2,'y'=8,'xh'=2,'c'=2] {'xl'}, use_global_device_ids=true, to_apply=%region_16.17 | all-reduce | flops 10752 | bytes 86016 | tf_op jit(solution)/shard_map/psum | solution.py:23
  173.9 29.7 %all-reduce.15 = (f32[5,1536]{1,0:T(8,128)S(1)}, f32[2,1536]{1,0:T(2,128)S(1)}) all-reduce(f32[5,1536]{1,0:T(8,128)S(1)} %get-tuple-element.26, f32[2,1536]{1,0:T(2,128)S(1)} %get-tuple-element.27), channel_id=1, replica_groups=mesh['z'=8,'xl'=2,'y'=8,'xh'=2,'c'=2] {'y'}, use_global_device_ids=true, to_apply=%region_17.18 | all-reduce | flops 10752 | bytes 86016 | tf_op jit(solution)/shard_map/psum | solution.py:23
  203.6 30.7 %all-reduce.16 = (f32[5,1536]{1,0:T(8,128)S(1)}, f32[2,1536]{1,0:T(2,128)S(1)}) all-reduce(f32[5,1536]{1,0:T(8,128)S(1)} %get-tuple-element.18, f32[2,1536]{1,0:T(2,128)S(1)} %get-tuple-element.19), channel_id=1, replica_groups=mesh['z'=8,'xl'=2,'y'=8,'xh'=2,'c'=2] {'z'}, use_global_device_ids=true, to_apply=%region_18.19 | all-reduce | flops 10752 | bytes 86016 | tf_op jit(solution)/shard_map/psum | solution.py:23
  234.3 1.3 add_convert_fusion
  236.9 2.3 all_to_all.18
  239.2 1.8 gather_fusion.1
  (61 shorter events, 9.5 us)
Async XLA Ops:
  7.2 36.9 %copy-start.8 = (s32[1,160]{1,0:T(1,128)S(1)}, s32[1,160]{1,0:T(1,128)}, u32[]{:S(2)}) copy-start(s32[1,160]{1,0:T(1,128)} %param.12) | copy-start | bytes 1924
  7.2 114.0 %all-gather.3.cloned.1.call-start = ((), (), s32[]{:S(2)}) async-start(), calls=%async_computation.2 | async-start | bytes 5308416 | tf_op jit(solution)/shard_map/all_gather | solution.py:18
  46.2 15.7 %copy-start.11 = (s32[1,8]{1,0:T(1,128)S(1)}, s32[1,8]{1,0:T(1,128)}, u32[]{:S(2)}) copy-start(s32[1,8]{1,0:T(1,128)} %param.10) | copy-start | bytes 100
  46.2 16.5 %copy-start.9 = (s32[1,256]{1,0:T(1,128)S(1)}, s32[1,256]{1,0:T(1,128)}, u32[]{:S(2)}) copy-start(s32[1,256]{1,0:T(1,128)} %param.11) | copy-start | bytes 3076
  46.2 16.6 %copy-start.6 = (f32[5,1536]{1,0:T(8,128)S(1)}, f32[5,1536]{1,0:T(8,128)}, u32[]{:S(2)}) copy-start(f32[5,1536]{1,0:T(8,128)} %param.13) | copy-start | bytes 92164
  46.3 17.4 %copy-start.4 = (bf16[256,3072]{1,0:T(8,128)(2,1)S(1)}, bf16[256,3072]{1,0:T(8,128)(2,1)}, u32[]{:S(2)}) copy-start(bf16[256,3072]{1,0:T(8,128)(2,1)} %param.9) | copy-start | bytes 4718596
  47.5 32.6 %all-to-all-start.1 = ((bf16[128,2,1536]{2,1,0:T(2,128)(2,1)}), bf16[128,2,1536]{2,1,0:T(2,128)(2,1)S(1)}, u32[]{:S(2)}, u32[]{:S(2)}) async-start(bf16[128,2,1536]{2,1,0:T(2,128)(2,1)} %all_to_all.19), calls=%async_computation.1 | async-start | bytes 1572864 | tf_op jit(solution)/shard_map/all_to_all | solution.py:89
  64.0 1.7 copy-start
  65.7 1.6 copy-start.2
  67.6 53.5 %copy-start.7 = (f32[1536]{0:T(1024)S(1)}, f32[1536]{0:T(1024)}, u32[]{:S(2)}) copy-start(f32[1536]{0:T(1024)} %param.14) | copy-start | bytes 18436
  67.6 53.5 %copy-start.10 = (f32[1536]{0:T(1024)S(1)}, f32[1536]{0:T(1024)}, u32[]{:S(2)}) copy-start(f32[1536]{0:T(1024)} %param.15) | copy-start | bytes 18436
  126.4 11.6 %copy-start.5 = (bf16[257,1536]{1,0:T(8,128)(2,1)S(1)}, bf16[257,1536]{1,0:T(8,128)(2,1)}, u32[]{:S(2)}) copy-start(bf16[257,1536]{1,0:T(8,128)(2,1)} %scatter_custom_fusion.1) | copy-start | bytes 2368516
  127.7 109.2 %all-to-all-start = ((bf16[128,2,1536]{2,1,0:T(2,128)(2,1)}), bf16[128,2,1536]{2,1,0:T(2,128)(2,1)}, u32[]{:S(2)}, u32[]{:S(2)}) async-start(bf16[128,2,1536]{2,1,0:T(2,128)(2,1)} %all_to_all.16), calls=%async_computation | async-start | bytes 1572864 | tf_op jit(solution)/shard_map/all_to_all | solution.py:86
  142.7 1.4 copy-start.3
  146.5 1.9 copy-start.1
Sparse Core Ops, SparseCore 0:
  44.2 76.8 all-gather.2

commit v2 on v1

--- a/solution.py
+++ b/solution.py
@@ -13,15 +13,20 @@
 
 
 def gather_weight(w):
-    w = lax.all_gather(w, "y", axis=0, tiled=True)
+    n_y = lax.axis_size("y")
+    copies = jnp.broadcast_to(w[None], (n_y,) + w.shape).reshape(n_y * w.shape[0], w.shape[1])
+    w = lax.all_to_all(copies, "y", 0, 0, tiled=True)
     w = lax.all_gather(w, "xl", axis=0, tiled=True)
     return lax.all_gather(w, "z", axis=0, tiled=True)
 
 
-def sum_all(tree):
-    for axis in ("c", "xh", "xl", "y", "z"):
-        tree = lax.psum(tree, axis)
-    return tree
+def sum_all(parts):
+    n_f = lax.axis_size(FSDP)
+    flat = parts.reshape(n_f, -1)
+    mine = lax.all_to_all(flat, FSDP, 0, 0, tiled=True).sum(0, keepdims=True)
+    mine = lax.psum(lax.psum(mine, "c"), "xh")
+    whole = lax.all_to_all(jnp.broadcast_to(mine, flat.shape), FSDP, 0, 0, tiled=True)
+    return whole.reshape(parts.shape)
 
 
 def conv_module(glu_rows, counts, kernel, gain_vec, bias_vec):
@@ -74,19 +79,18 @@
 
     activated, pullback = jax.vjp(local_pass, glu_input, depth_kernel, norm_gain, norm_bias)
     activations = activated.astype(jnp.bfloat16)
-    full_weight = gather_weight(point_weight)
-    produced = jnp.dot(
-        activations,
-        full_weight,
-        preferred_element_type=jnp.float32,
-    ).astype(jnp.bfloat16)
-    outgoing = jnp.concatenate([produced, jnp.zeros((1, out_count), jnp.bfloat16)], axis=0)[
+    outgoing = jnp.concatenate([activations, jnp.zeros((1, out_count), jnp.bfloat16)], axis=0)[
         send_slot
     ]
-    arrived = lax.all_to_all(outgoing, FSDP, split_axis=0, concat_axis=0, tiled=True)
-    output = arrived[owner_slot]
     parked = jnp.zeros((row_count, out_count), jnp.bfloat16).at[owner_slot].set(cotangent)
-    returned = lax.all_to_all(parked, FSDP, split_axis=0, concat_axis=0, tiled=True)
+    moved = lax.all_to_all(
+        jnp.concatenate([outgoing, parked], axis=1), FSDP, split_axis=0, concat_axis=0, tiled=True
+    )
+    arrived, returned = moved[:, :out_count], moved[:, out_count:]
+    full_weight = gather_weight(point_weight)
+    output = jnp.dot(
+        arrived[owner_slot], full_weight, preferred_element_type=jnp.float32
+    ).astype(jnp.bfloat16)
     home_rows = (
         jnp.zeros((row_count + 1, out_count), jnp.bfloat16).at[send_slot].set(returned)[:row_count]
     )
@@ -97,7 +101,8 @@
         preferred_element_type=jnp.float32,
     ).astype(jnp.bfloat16)
     input_grad, kernel_part, gain_part, bias_part = pullback(grad_acts.astype(jnp.float32))
-    totals = sum_all((kernel_part, jnp.stack([gain_part, bias_part])))
+    totals = sum_all(jnp.concatenate([kernel_part, gain_part[None], bias_part[None]], axis=0))
+    totals = (totals[: kernel_part.shape[0]], totals[kernel_part.shape[0] :])
     frame_total = owner_slot.shape[0] * lax.axis_size(ALL)
     grad_scale = 1.0 / math.sqrt(frame_total)
     return (output, input_grad, totals[0] * grad_scale, totals[1] * grad_scale)

time: 248 us -> 212 us (0.85)
  the two profiles are of different devices: /device:TPU:2 before, /device:TPU:1 now
where the time goes in v2:
time: 212 us; the launch traced here: 210 us
  waiting for transfers between devices  78.9 us (37%)
  blocking collectives  37.4 us (18%)
  starting transfers between devices  33.9 us (16%)
  local copies, waits for them, and re-layouts  20.1 us (9%)
  other arithmetic  16.5 us (8%)
  between operations  14.4 us (7%)
  matrix products  8.82 us (4%)
    all_to_all x1, waiting for transfers between devices, per_device(): lax.all_to_all(jnp.concatenate([outgoing, parked], axis=1), FSDP, split_a...  39.1 us
    all_gather x1, waiting for transfers between devices, gather_weight(): return lax.all_gather(w, 'z', axis=0, tiled=True)  22.3 us
    all_to_all x1, blocking collectives, gather_weight(): w = lax.all_to_all(copies, 'y', 0, 0, tiled=True)  20 us
    all_to_all x1, starting transfers between devices, per_device(): lax.all_to_all(jnp.concatenate([outgoing, parked], axis=1), FSDP, split_a...  15.8 us
    all_to_all x1, starting transfers between devices, sum_all(): mine = lax.all_to_all(flat, FSDP, 0, 0, tiled=True).sum(0, keepdims=True)  11.9 us
    all_to_all x1, waiting for transfers between devices, sum_all(): lax.all_to_all(jnp.broadcast_to(mine, flat.shape), FSDP, 0, 0, tiled=True)  10.2 us
    psum x2, blocking collectives, sum_all(): mine = lax.psum(lax.psum(mine, 'c'), 'xh')  9.63 us
    all_gather x1, blocking collectives, gather_weight(): w = lax.all_gather(w, 'xl', axis=0, tiled=True)  7.79 us
  transfers between devices with their start and end apart: 4, of which 4 were waited for; matrix products, arithmetic and copies ran while one was open for 12% of the time, Pallas kernels for 0%

profile of v2, /device:TPU:1, one launch (start us, length us, event | category | flops | bytes accessed | tf_op | source)
XLA Modules:
  0.0 210.0 jit_solution(12704888493649700605)
XLA Ops:
  8.0 20.0 %all_to_all.36 = bf16[8,12,1536]{2,1,0:T(8,128)(2,1)S(1)} all-to-all(bf16[8,12,1536]{2,1,0:T(8,128)(2,1)S(1)} %broadcast_in_dim.108), channel_id=1, replica_groups=mesh['z'=8,'xl'=2,'y'=8,'xh'=2,'c'=2] {'y'}, dimensions={0} | all-to-all | bytes 589824 | tf_op jit(solution)/shard_map/all_to_all | solution.py:18
  28.1 7.8 %all_gather.6 = bf16[192,1536]{1,0:T(8,128)(2,1)} all-gather(bf16[96,1536]{1,0:T(8,128)(2,1)S(1)} %all_to_all.28), channel_id=1, replica_groups=mesh['z'=8,'xl'=2,'y'=8,'xh'=2,'c'=2] {'xl'}, dimensions={0}, use_global_device_ids=true | all-gather | bytes 884736 | tf_op jit(solution)/shard_map/all_gather | solution.py:19
  35.9 1.8 convert_element_type.24
  40.1 1.7 fusion.22
  43.5 2.8 %scatter_custom_fusion = bf16[256,1536]{1,0:T(8,128)(2,1)} fusion(s32[160]{0:T(256)S(1)} %bitcast.17, bf16[160,1536]{1,0:T(8,128)(2,1)} %param.17, bf16[]{:T(256)} %constant.43.clone.1), kind=kCustom, calls=%fused_computation.53 | custom fusion | bytes 786944 | tf_op jit(solution)/shard_map/scatter | solution.py:85
  46.3 2.1 %gather_fusion = bf16[256,1536]{1,0:T(8,128)(2,1)} fusion(bf16[257,1536]{1,0:T(8,128)(2,1)S(1)} %concatenate.9, s32[1024]{0:T(1024)S(1)} %pad_clamp_fusion.1), kind=kCustom, calls=%fused_computation | custom fusion | bytes 1573888 | tf_op jit(solution)/shard_map/gather | solution.py:82
  48.4 1.5 pad_maximum_fusion
  50.0 1.5 all_to_all.24
  51.5 15.8 %all-to-all-start = ((bf16[128,2,3072]{2,1,0:T(2,128)(2,1)}), bf16[128,2,3072]{2,1,0:T(2,128)(2,1)S(1)}, u32[]{:S(2)}, u32[]{:S(2)}) async-start(bf16[128,2,3072]{2,1,0:T(2,128)(2,1)} %all_to_all.24), calls=%async_computation | async-start | bytes 3145728 | tf_op jit(solution)/shard_map/all_to_all | solution.py:86
  67.3 39.1 %all-to-all-done = bf16[128,2,3072]{2,1,0:T(2,128)(2,1)S(1)} async-done(((bf16[128,2,3072]{2,1,0:T(2,128)(2,1)}), bf16[128,2,3072]{2,1,0:T(2,128)(2,1)S(1)}, u32[]{:S(2)}, u32[]{:S(2)}) %all-to-all-start) | async-done | bytes 1572896 | tf_op jit(solution)/shard_map/all_to_all | solution.py:86
  106.3 1.5 all_to_all.26
  109.0 2.8 %scatter_custom_fusion.1 = bf16[257,1536]{1,0:T(8,128)(2,1)S(1)} fusion(s32[256]{0:T(256)S(1)} %bitcast.16, bf16[256,3072]{1,0:T(8,128)(2,1)} %all_to_all.26, bf16[]{:T(256)} %constant.43.clone.1), kind=kCustom, calls=%fused_computation.49 | custom fusion | bytes 1576448 | tf_op jit(solution)/shard_map/scatter | solution.py:95
  111.8 1.8 gather_fusion.1
  113.6 22.3 %all-gather.2.cloned.1.call-done = bf16[1536,1536]{1,0:T(8,128)(2,1)} async-done(((bf16[192,1536]{1,0:T(8,128)(2,1)}), bf16[1536,1536]{1,0:T(8,128)(2,1)}) %all-gather.2.cloned.1.call-update) | async-done | bytes 4718608 | tf_op jit(solution)/shard_map/all_gather | solution.py:20
  135.9 4.6 %multiply_reduce_fusion = (f32[1536]{0:T(1024)S(1)}, f32[256]{0:T(256)S(1)}, f32[256]{0:T(256)S(1)}, f32[1536]{0:T(1024)S(1)}, f32[256,1536]{1,0:T(8,128)S(1)}) fusion(f32[256,1536]{1,0:T(8,128)S(1)} %get-tuple-element.22, f32[256]{0:T(256)S(1)} %fusion.19, f32[256]{0:T(256)S(1)} %broadcast_multiply_fusion.1, f32[1536]{0:T(1024)S(1)} %copy-done.4, ...), kind=kOutput, calls=%fused_computation.24 | convolution fusion | flops 1217393152 | bytes 8684032 | tf_op jit(solution)/shard_map/dot_general | solution.py:97
  141.9 2.4 %multiply_reduce_fusion.5 = (f32[1536]{0:T(1024)S(1)}, f32[1536]{0:T(1024)S(1)}, f32[1536]{0:T(1024)S(1)}, f32[1536]{0:T(1024)S(1)}, f32[1536]{0:T(1024)S(1)}, /*index=5*/f32[256,1536]{1,0:T(8,128)S(1)}) fusion(f32[256,1536]{1,0:T(8,128)S(1)} %copy-done.3, pred[256]{0:T(512)(128)(4,1)S(1)} %get-tuple-element.31, pred[256]{0:T(512)(128)(4,1)S(1)} %get-tuple-element.28, ...), kind=kLoop, calls=%fused_computation.29 | loop fusion | flops 7856640 | bytes 6333440 | tf_op jit(solution)/shard_map/transpose(jvp())/reduce_sum | solution.py:50
  146.2 1.4 fusion.4
  148.9 11.9 %all-to-all-start.2 = ((f32[128,1,84]{2,1,0:T(1,128)}), f32[128,1,84]{2,1,0:T(1,128)S(1)}, u32[]{:S(2)}, u32[]{:S(2)}) async-start(f32[128,1,84]{2,1,0:T(1,128)} %bitcast.7), calls=%async_computation.2 | async-start | bytes 131072 | tf_op jit(solution)/shard_map/all_to_all | solution.py:26
  160.8 4.2 %convolution_convert_fusion.1 = bf16[160,1536]{1,0:T(8,128)(2,1)} fusion(bf16[160,1536]{1,0:T(8,128)(2,1)} %gather_fusion.1, bf16[1536,1536]{1,0:T(8,128)(2,1)} %all-gather.2.cloned.1.call-done), kind=kOutput, calls=%fused_computation.8 | convolution fusion | flops 755220480 | bytes 5701632 | tf_op jit(solution)/shard_map/dot_general | solution.py:91
  165.0 7.3 %all-to-all-done.2 = f32[128,1,84]{2,1,0:T(1,128)S(1)} async-done(((f32[128,1,84]{2,1,0:T(1,128)}), f32[128,1,84]{2,1,0:T(1,128)S(1)}, u32[]{:S(2)}, u32[]{:S(2)}) %all-to-all-start.2) | async-done | bytes 43040 | tf_op jit(solution)/shard_map/all_to_all | solution.py:26
  172.5 4.4 %psum.16 = f32[1,84]{1,0:T(1,128)S(1)} all-reduce(f32[1,84]{1,0:T(1,128)S(1)} %bitcast.19), channel_id=1, replica_groups=mesh['z'=8,'xl'=2,'y'=8,'xh'=2,'c'=2] {'c'}, use_global_device_ids=true, to_apply=%region_17.18 | all-reduce | flops 84 | bytes 672 | tf_op jit(solution)/shard_map/psum | solution.py:27
  176.9 5.3 %psum.18 = f32[84]{0:T(128)S(1)} all-reduce(f32[84]{0:T(128)S(1)} %bitcast.22), channel_id=1, replica_groups=mesh['z'=8,'xl'=2,'y'=8,'xh'=2,'c'=2] {'xh'}, use_global_device_ids=true, to_apply=%region_18.19 | all-reduce | flops 84 | bytes 672 | tf_op jit(solution)/shard_map/psum | solution.py:27
  182.8 6.2 %all-to-all-start.3 = ((f32[128,1,84]{2,1,0:T(1,128)}), f32[128,1,84]{2,1,0:T(1,128)S(1)}, u32[]{:S(2)}, u32[]{:S(2)}) async-start(f32[128,1,84]{2,1,0:T(1,128)} %broadcast_in_dim.112), calls=%async_computation.3 | async-start | bytes 131072 | tf_op jit(solution)/shard_map/all_to_all | solution.py:28
  190.3 10.2 %all-to-all-done.3 = f32[128,1,84]{2,1,0:T(1,128)S(1)} async-done(((f32[128,1,84]{2,1,0:T(1,128)}), f32[128,1,84]{2,1,0:T(1,128)S(1)}, u32[]{:S(2)}, u32[]{:S(2)}) %all-to-all-start.3) | async-done | bytes 43040 | tf_op jit(solution)/shard_map/all_to_all | solution.py:28
  (64 shorter events, 15.4 us)
Async XLA Ops:
  7.2 128.7 %all-gather.2.cloned.1.call-start = ((), (), s32[]{:S(2)}) async-start(), calls=%async_computation.4 | async-start | bytes 5308416 | tf_op jit(solution)/shard_map/all_gather | solution.py:20
  35.9 1.8 copy-start.9
  35.9 3.6 %copy-start.5 = (f32[5,1536]{1,0:T(8,128)S(1)}, f32[5,1536]{1,0:T(8,128)}, u32[]{:S(2)}) copy-start(f32[5,1536]{1,0:T(8,128)} %param.13) | copy-start | bytes 92164
  37.7 2.4 %copy-start = (f32[256,3072]{1,0:T(8,128)}, f32[256,3072]{1,0:T(8,128)S(1)}, u32[]{:S(2)}) copy-start(f32[256,3072]{1,0:T(8,128)S(1)} %convert_element_type.24) | copy-start | bytes 9437188
  40.1 1.7 copy-start.2
  41.8 0.7 copy-start.4
  41.8 0.7 copy-start.6
  42.5 0.9 copy-start.7
  43.4 2.9 %copy-start.8 = (s32[1,256]{1,0:T(1,128)S(1)}, s32[1,256]{1,0:T(1,128)}, u32[]{:S(2)}) copy-start(s32[1,256]{1,0:T(1,128)} %param.11) | copy-start | bytes 3076
  51.5 54.9 %all-to-all-start = ((bf16[128,2,3072]{2,1,0:T(2,128)(2,1)}), bf16[128,2,3072]{2,1,0:T(2,128)(2,1)S(1)}, u32[]{:S(2)}, u32[]{:S(2)}) async-start(bf16[128,2,3072]{2,1,0:T(2,128)(2,1)} %all_to_all.24), calls=%async_computation | async-start | bytes 3145728 | tf_op jit(solution)/shard_map/all_to_all | solution.py:86
  140.5 1.4 copy-start.3
  144.3 1.9 copy-start.1
  148.9 23.4 %all-to-all-start.2 = ((f32[128,1,84]{2,1,0:T(1,128)}), f32[128,1,84]{2,1,0:T(1,128)S(1)}, u32[]{:S(2)}, u32[]{:S(2)}) async-start(f32[128,1,84]{2,1,0:T(1,128)} %bitcast.7), calls=%async_computation.2 | async-start | bytes 131072 | tf_op jit(solution)/shard_map/all_to_all | solution.py:26
  182.8 17.7 %all-to-all-start.3 = ((f32[128,1,84]{2,1,0:T(1,128)}), f32[128,1,84]{2,1,0:T(1,128)S(1)}, u32[]{:S(2)}, u32[]{:S(2)}) async-start(f32[128,1,84]{2,1,0:T(1,128)} %broadcast_in_dim.112), calls=%async_computation.3 | async-start | bytes 131072 | tf_op jit(solution)/shard_map/all_to_all | solution.py:28
Sparse Core Ops, SparseCore 0:
  36.0 99.8 all-gather.1

commit v3 on v2

--- a/solution.py
+++ b/solution.py
@@ -12,12 +12,22 @@
 ALL = FSDP + DP
 
 
-def gather_weight(w):
+def gather_over_fsdp(w):
     n_y = lax.axis_size("y")
     copies = jnp.broadcast_to(w[None], (n_y,) + w.shape).reshape(n_y * w.shape[0], w.shape[1])
     w = lax.all_to_all(copies, "y", 0, 0, tiled=True)
     w = lax.all_gather(w, "xl", axis=0, tiled=True)
     return lax.all_gather(w, "z", axis=0, tiled=True)
+
+
+def gather_weight(w):
+    width = w.shape[1] // 2
+    core = lax.axis_index("c")
+    mine = gather_over_fsdp(lax.dynamic_slice_in_dim(w, core * width, width, axis=1))
+    other = lax.ppermute(mine, "c", [(0, 1), (1, 0)])
+    return jnp.where(
+        core == 0, jnp.concatenate([mine, other], axis=1), jnp.concatenate([other, mine], axis=1)
+    )
 
 
 def sum_all(parts):

time: 212 us -> 207 us (0.976)
  blocking collectives: 37.4 us -> 12.5 us
  starting transfers between devices: 33.9 us -> 55.2 us
  waiting for transfers between devices: 78.9 us -> 60.2 us
  other arithmetic: 16.5 us -> 29.4 us
  matrix products: 8.82 us -> 12.2 us
    all_to_all x1, waiting for transfers between devices: 39.1 us -> 0.01 us  [per_device(): lax.all_to_all(jnp.concatenate([outgoing, parked], axis=1), FSDP, split_a...]
    all_gather x1, waiting for transfers between devices: 22.3 us -> 48.1 us  [gather_over_fsdp(): return lax.all_gather(w, 'z', axis=0, tiled=True)]
    all_to_all x1 -> x0, blocking collectives: 20 us -> none  [gather_weight(): w = lax.all_to_all(copies, 'y', 0, 0, tiled=True)]
    all_to_all x1, starting transfers between devices: 6.17 us -> 14.3 us  [sum_all(): lax.all_to_all(jnp.broadcast_to(mine, flat.shape), FSDP, 0, 0, tiled=True)]
    all_to_all x0 -> x1, starting transfers between devices: none -> 7.64 us  [gather_over_fsdp(): w = lax.all_to_all(copies, 'y', 0, 0, tiled=True)]
    all_to_all x1, waiting for transfers between devices: 7.32 us -> 0.01 us  [sum_all(): mine = lax.all_to_all(flat, FSDP, 0, 0, tiled=True).sum(0, keepdims=True)]
    ppermute x0 -> x1, starting transfers between devices: none -> 6.02 us  [gather_weight(): other = lax.ppermute(mine, 'c', [(0, 1), (1, 0)])]
    mul x2, other arithmetic: 1.81 us -> 7.53 us  [conv_module(): mixed_vals = values[:, :chan_count] * jax.nn.sigmoid(values[:, chan_count:])]
  transfers between devices with their start and end apart: 4 -> 6, of which waited for: 4 -> 3; matrix products, arithmetic and copies ran while one was open for 12% -> 19% of each run, Pallas kernels for 0% -> 0%
where the time goes in v3:
time: 207 us; the launch traced here: 204 us
  waiting for transfers between devices  60.2 us (29%)
  starting transfers between devices  55.2 us (27%)
  other arithmetic  29.4 us (14%)
  local copies, waits for them, and re-layouts  20.5 us (10%)
  between operations  14.4 us (7%)
  blocking collectives  12.5 us (6%)
  matrix products  12.2 us (6%)
    all_gather x1, waiting for transfers between devices, gather_over_fsdp(): return lax.all_gather(w, 'z', axis=0, tiled=True)  48.1 us
    all_to_all x1, starting transfers between devices, per_device(): lax.all_to_all(jnp.concatenate([outgoing, parked], axis=1), FSDP, split_a...  15.2 us
    all_to_all x1, starting transfers between devices, sum_all(): lax.all_to_all(jnp.broadcast_to(mine, flat.shape), FSDP, 0, 0, tiled=True)  14.3 us
    all_to_all x1, starting transfers between devices, sum_all(): mine = lax.all_to_all(flat, FSDP, 0, 0, tiled=True).sum(0, keepdims=True)  11.9 us
    all_to_all x1, waiting for transfers between devices, sum_all(): lax.all_to_all(jnp.broadcast_to(mine, flat.shape), FSDP, 0, 0, tiled=True)  8.3 us
    psum x2, blocking collectives, sum_all(): mine = lax.psum(lax.psum(mine, 'c'), 'xh')  7.73 us
    all_to_all x1, starting transfers between devices, gather_over_fsdp(): w = lax.all_to_all(copies, 'y', 0, 0, tiled=True)  7.64 us
    mul x2, other arithmetic, conv_module(): mixed_vals = values[:, :chan_count] * jax.nn.sigmoid(values[:, chan_count:])  7.53 us
  transfers between devices with their start and end apart: 6, of which 3 were waited for; matrix products, arithmetic and copies ran while one was open for 19% of the time, Pallas kernels for 0%

profile of v3, /device:TPU:1, one launch (start us, length us, event | category | flops | bytes accessed | tf_op | source)
XLA Modules:
  0.0 204.4 jit_solution(2996623549303750850)
XLA Ops:
  8.7 7.6 %all-to-all-start.1 = ((bf16[8,12,768]{2,1,0:T(8,128)(2,1)}), bf16[8,12,768]{2,1,0:T(8,128)(2,1)S(1)}, u32[]{:S(2)}, u32[]{:S(2)}) async-start(bf16[8,12,768]{2,1,0:T(8,128)(2,1)} %broadcast_in_dim.108), calls=%async_computation.1 | async-start | bytes 393216 | tf_op jit(solution)/shard_map/all_to_all | solution.py:18
  17.2 1.8 convert_element_type.24
  21.2 3.9 %all-to-all-done.1 = bf16[8,12,768]{2,1,0:T(8,128)(2,1)S(1)} async-done(((bf16[8,12,768]{2,1,0:T(8,128)(2,1)}), bf16[8,12,768]{2,1,0:T(8,128)(2,1)S(1)}, u32[]{:S(2)}, u32[]{:S(2)}) %all-to-all-start.1) | async-done | bytes 147488 | tf_op jit(solution)/shard_map/all_to_all | solution.py:18
  25.1 4.8 %all_gather.6 = bf16[192,768]{1,0:T(8,128)(2,1)} all-gather(bf16[96,768]{1,0:T(8,128)(2,1)S(1)} %all_to_all.28), channel_id=1, replica_groups=mesh['z'=8,'xl'=2,'y'=8,'xh'=2,'c'=2] {'xl'}, dimensions={0}, use_global_device_ids=true | all-gather | bytes 442368 | tf_op jit(solution)/shard_map/all_gather | solution.py:19
  32.2 1.7 fusion.24
  35.6 2.8 %scatter_custom_fusion = bf16[256,1536]{1,0:T(8,128)(2,1)} fusion(s32[160]{0:T(256)S(1)} %bitcast.15, bf16[160,1536]{1,0:T(8,128)(2,1)} %param.17, bf16[]{:T(256)} %constant.48.clone.1), kind=kCustom, calls=%fused_computation.54 | custom fusion | bytes 786944 | tf_op jit(solution)/shard_map/scatter | solution.py:95
  38.4 2.2 %gather_fusion = bf16[256,1536]{1,0:T(8,128)(2,1)} fusion(bf16[257,1536]{1,0:T(8,128)(2,1)S(1)} %concatenate.15, s32[1024]{0:T(1024)S(1)} %pad_clamp_fusion.1), kind=kCustom, calls=%fused_computation | custom fusion | bytes 1573888 | tf_op jit(solution)/shard_map/gather | solution.py:92
  43.6 15.2 %all-to-all-start = ((bf16[128,2,3072]{2,1,0:T(2,128)(2,1)}), bf16[128,2,3072]{2,1,0:T(2,128)(2,1)S(1)}, u32[]{:S(2)}, u32[]{:S(2)}) async-start(bf16[128,2,3072]{2,1,0:T(2,128)(2,1)} %all_to_all.24), calls=%async_computation | async-start | bytes 3145728 | tf_op jit(solution)/shard_map/all_to_all | solution.py:96
  58.9 48.1 %all-gather.2.cloned.1.call-done = bf16[1536,768]{1,0:T(8,128)(2,1)} async-done(((bf16[192,768]{1,0:T(8,128)(2,1)}), bf16[1536,768]{1,0:T(8,128)(2,1)}) %all-gather.2.cloned.1.call-update) | async-done | bytes 2359312 | tf_op jit(solution)/shard_map/all_gather | solution.py:20
  106.9 6.0 %collective-permute-start = (bf16[1536,768]{1,0:T(8,128)(2,1)}, bf16[1536,768]{1,0:T(8,128)(2,1)}, u32[]{:S(2)}, u32[]{:S(2)}) collective-permute-start(bf16[1536,768]{1,0:T(8,128)(2,1)} %all-gather.2.cloned.1.call-done), channel_id=1, source_target_pairs={{0,1},{1,0},{2,3},{3,2},{4,5},{5,4},{6,7},{7,6},{8,9},{9,8},{10,11... | collective-permute-start | bytes 7077896 | tf_op jit(solution)/shard_map/ppermute | solution.py:27
  115.7 2.8 %scatter_custom_fusion.1 = bf16[257,1536]{1,0:T(8,128)(2,1)S(1)} fusion(s32[256]{0:T(256)S(1)} %bitcast.14, bf16[256,3072]{1,0:T(8,128)(2,1)} %all_to_all.26, bf16[]{:T(256)} %constant.48.clone.1), kind=kCustom, calls=%fused_computation.50 | custom fusion | bytes 1576448 | tf_op jit(solution)/shard_map/scatter | solution.py:105
  118.5 1.8 gather_fusion.1
  120.2 6.8 %multiply_reduce_fusion = (f32[1536]{0:T(1024)S(1)}, f32[256]{0:T(256)S(1)}, f32[256]{0:T(256)S(1)}, f32[1536]{0:T(1024)S(1)}, f32[256,1536]{1,0:T(8,128)S(1)}) fusion(f32[256,1536]{1,0:T(8,128)S(1)} %get-tuple-element.22, f32[256]{0:T(256)S(1)} %fusion.19, f32[256]{0:T(256)S(1)} %broadcast_multiply_fusion.1, f32[1536]{0:T(1024)S(1)} %copy-done.9, ...), kind=kOutput, calls=%fused_computation.25 | convolution fusion | flops 1238626816 | bytes 8684033 | tf_op jit(solution)/shard_map/dot_general | solution.py:107
  128.4 2.4 %multiply_reduce_fusion.5 = (f32[1536]{0:T(1024)S(1)}, f32[1536]{0:T(1024)S(1)}, f32[1536]{0:T(1024)S(1)}, f32[1536]{0:T(1024)S(1)}, f32[1536]{0:T(1024)S(1)}, /*index=5*/f32[256,1536]{1,0:T(8,128)S(1)}) fusion(f32[256,1536]{1,0:T(8,128)S(1)} %copy-done.4, pred[256]{0:T(512)(128)(4,1)S(1)} %get-tuple-element.31, pred[256]{0:T(512)(128)(4,1)S(1)} %get-tuple-element.28, ...), kind=kLoop, calls=%fused_computation.30 | loop fusion | flops 7856640 | bytes 6333440 | tf_op jit(solution)/shard_map/transpose(jvp())/reduce_sum | solution.py:60
  130.8 3.9 %multiply_select_fusion.3 = (f32[256,1536]{1,0:T(8,128)}, f32[256,1536]{1,0:T(8,128)}, f32[256,1536]{1,0:T(8,128)}, f32[256,1536]{1,0:T(8,128)}, f32[256,1536]{1,0:T(8,128)}) fusion(f32[256,1536]{1,0:T(8,128)S(1)} %get-tuple-element.18, f32[1536]{0:T(1024)S(1)} %copy-done.7, pred[256]{0:T(512)(128)(4,1)S(1)} %get-tuple-element.31, ...), kind=kLoop, calls=%fused_computation.34 | loop fusion | flops 3538944 | bytes 9468928 | tf_op jit(solution)/shard_map/transpose(jvp(jit(_where)))/select_n | solution.py:60
  135.6 11.9 %all-to-all-start.2 = ((f32[128,1,84]{2,1,0:T(1,128)}), f32[128,1,84]{2,1,0:T(1,128)S(1)}, u32[]{:S(2)}, u32[]{:S(2)}) async-start(f32[128,1,84]{2,1,0:T(1,128)} %bitcast.7), calls=%async_computation.2 | async-start | bytes 131072 | tf_op jit(solution)/shard_map/all_to_all | solution.py:36
  147.5 6.0 %fusion.4 = (f32[256,1536]{1,0:T(8,128)}, f32[256,1536]{1,0:T(8,128)S(1)}) fusion(f32[256,3072]{1,0:T(8,128)S(1)} %copy-done.2, f32[256,1536]{1,0:T(8,128)} %get-tuple-element.24, f32[256,1536]{1,0:T(8,128)} %get-tuple-element.25, f32[256,1536]{1,0:T(8,128)} %get-tuple-element.26, f32[256,1536]{1,0:T(8,128)} %get-tuple-element.27, ...), kind=kLoop, calls=%fused_computation.14 | loop fusion | flops 4718592 | bytes 14156032 | tf_op jit(solution)/shard_map/transpose(jvp())/mul | solution.py:47
  153.5 5.4 %convolution_convert_fusion.1 = bf16[160,1536]{1,0:T(8,128)(2,1)} fusion(bf16[160,1536]{1,0:T(8,128)(2,1)S(1)} %copy-done.5, bf16[1536,768]{1,0:T(8,128)(2,1)} %collective-permute-done, bf16[1536,768]{1,0:T(8,128)(2,1)S(1)} %copy-done.14, pred[]{:T(512)S(6)} %eq.20), kind=kOutput, calls=%fused_computation.9 | convolution fusion | flops 776454144 | bytes 5701633 | tf_op jit(solution)/shard_map/dot_general | solution.py:101
  159.0 1.6 fusion.22
  160.7 2.5 %psum.16 = f32[1,84]{1,0:T(1,128)S(1)} all-reduce(f32[1,84]{1,0:T(1,128)S(1)} %bitcast.17), channel_id=1, replica_groups=mesh['z'=8,'xl'=2,'y'=8,'xh'=2,'c'=2] {'c'}, use_global_device_ids=true, to_apply=%region_17.18 | all-reduce | flops 84 | bytes 672 | tf_op jit(solution)/shard_map/psum | solution.py:37
  163.1 5.3 %psum.18 = f32[84]{0:T(128)S(1)} all-reduce(f32[84]{0:T(128)S(1)} %bitcast.20), channel_id=1, replica_groups=mesh['z'=8,'xl'=2,'y'=8,'xh'=2,'c'=2] {'xh'}, use_global_device_ids=true, to_apply=%region_18.19 | all-reduce | flops 84 | bytes 672 | tf_op jit(solution)/shard_map/psum | solution.py:37
  169.1 14.3 %all-to-all-start.3 = ((f32[128,1,84]{2,1,0:T(1,128)}), f32[128,1,84]{2,1,0:T(1,128)S(1)}, u32[]{:S(2)}, u32[]{:S(2)}) async-start(f32[128,1,84]{2,1,0:T(1,128)} %broadcast_in_dim.112), calls=%async_computation.3 | async-start | bytes 131072 | tf_op jit(solution)/shard_map/all_to_all | solution.py:38
  183.4 3.2 %add_convert_fusion = bf16[256,3072]{1,0:T(8,128)(2,1)} fusion(f32[256,1536]{1,0:T(8,128)} %fusion.22, f32[256,1536]{1,0:T(8,128)} %get-tuple-element.19), kind=kLoop, calls=%fused_computation.5 | loop fusion | flops 1572864 | bytes 4718592 | tf_op jit(solution)/shard_map/transpose(jvp())/convert_element_type | solution.py:46
  186.6 8.3 %all-to-all-done.3 = f32[128,1,84]{2,1,0:T(1,128)S(1)} async-done(((f32[128,1,84]{2,1,0:T(1,128)}), f32[128,1,84]{2,1,0:T(1,128)S(1)}, u32[]{:S(2)}, u32[]{:S(2)}) %all-to-all-start.3) | async-done | bytes 43040 | tf_op jit(solution)/shard_map/all_to_all | solution.py:38
  (78 shorter events, 20.0 us)
Async XLA Ops:
  7.2 0.8 copy-start
  8.7 16.4 %all-to-all-start.1 = ((bf16[8,12,768]{2,1,0:T(8,128)(2,1)}), bf16[8,12,768]{2,1,0:T(8,128)(2,1)S(1)}, u32[]{:S(2)}, u32[]{:S(2)}) async-start(bf16[8,12,768]{2,1,0:T(8,128)(2,1)} %broadcast_in_dim.108), calls=%async_computation.1 | async-start | bytes 393216 | tf_op jit(solution)/shard_map/all_to_all | solution.py:18
  16.3 90.6 %all-gather.2.cloned.1.call-start = ((), (), s32[]{:S(2)}) async-start(), calls=%async_computation.4 | async-start | bytes 2654208 | tf_op jit(solution)/shard_map/all_gather | solution.py:20
  17.2 3.3 %copy-start.10 = (f32[5,1536]{1,0:T(8,128)S(1)}, f32[5,1536]{1,0:T(8,128)}, u32[]{:S(2)}) copy-start(f32[5,1536]{1,0:T(8,128)} %param.13) | copy-start | bytes 92164
  19.0 13.0 %copy-start.1 = (f32[256,3072]{1,0:T(8,128)}, f32[256,3072]{1,0:T(8,128)S(1)}, u32[]{:S(2)}) copy-start(f32[256,3072]{1,0:T(8,128)S(1)} %convert_element_type.24) | copy-start | bytes 9437188
  31.5 0.7 copy-start.6
  31.5 0.7 copy-start.7
  31.5 0.7 copy-start.8
  31.9 2.0 copy-start.3
  33.9 0.7 copy-start.9
  33.9 0.7 copy-start.11
  34.6 1.0 copy-start.12
  35.5 2.9 %copy-start.13 = (s32[1,256]{1,0:T(1,128)S(1)}, s32[1,256]{1,0:T(1,128)}, u32[]{:S(2)}) copy-start(s32[1,256]{1,0:T(1,128)} %param.11) | copy-start | bytes 3076
  43.6 69.3 %all-to-all-start = ((bf16[128,2,3072]{2,1,0:T(2,128)(2,1)}), bf16[128,2,3072]{2,1,0:T(2,128)(2,1)S(1)}, u32[]{:S(2)}, u32[]{:S(2)}) async-start(bf16[128,2,3072]{2,1,0:T(2,128)(2,1)} %all_to_all.24), calls=%async_computation | async-start | bytes 3145728 | tf_op jit(solution)/shard_map/all_to_all | solution.py:96
  106.9 13.3 %collective-permute-start = (bf16[1536,768]{1,0:T(8,128)(2,1)}, bf16[1536,768]{1,0:T(8,128)(2,1)}, u32[]{:S(2)}, u32[]{:S(2)}) collective-permute-start(bf16[1536,768]{1,0:T(8,128)(2,1)} %all-gather.2.cloned.1.call-done), channel_id=1, source_target_pairs={{0,1},{1,0},{2,3},{3,2},{4,5},{5,4},{6,7},{7,6},{8,9},{9,8},{10,11... | collective-permute-start | bytes 7077896 | tf_op jit(solution)/shard_map/ppermute | solution.py:27
  127.0 1.4 copy-start.4
  130.8 16.7 %copy-start.2 = (f32[256,3072]{1,0:T(8,128)S(1)}, f32[256,3072]{1,0:T(8,128)}, u32[]{:S(2)}) copy-start(f32[256,3072]{1,0:T(8,128)} %copy-done.1) | copy-start | bytes 9437188
  135.6 24.9 %all-to-all-start.2 = ((f32[128,1,84]{2,1,0:T(1,128)}), f32[128,1,84]{2,1,0:T(1,128)S(1)}, u32[]{:S(2)}, u32[]{:S(2)}) async-start(f32[128,1,84]{2,1,0:T(1,128)} %bitcast.7), calls=%async_computation.2 | async-start | bytes 131072 | tf_op jit(solution)/shard_map/all_to_all | solution.py:36
  147.5 6.0 %copy-start.5 = (bf16[160,1536]{1,0:T(8,128)(2,1)S(1)}, bf16[160,1536]{1,0:T(8,128)(2,1)}, u32[]{:S(2)}) copy-start(bf16[160,1536]{1,0:T(8,128)(2,1)} %gather_fusion.1) | copy-start | bytes 1474564
  147.5 6.0 %copy-start.14 = (bf16[1536,768]{1,0:T(8,128)(2,1)S(1)}, bf16[1536,768]{1,0:T(8,128)(2,1)}, u32[]{:S(2)}) copy-start(bf16[1536,768]{1,0:T(8,128)(2,1)} %all-gather.2.cloned.1.call-done) | copy-start | bytes 7077892
  169.1 25.8 %all-to-all-start.3 = ((f32[128,1,84]{2,1,0:T(1,128)}), f32[128,1,84]{2,1,0:T(1,128)S(1)}, u32[]{:S(2)}, u32[]{:S(2)}) async-start(f32[128,1,84]{2,1,0:T(1,128)} %broadcast_in_dim.112), calls=%async_computation.3 | async-start | bytes 131072 | tf_op jit(solution)/shard_map/all_to_all | solution.py:38
Sparse Core Ops, SparseCore 0:
  30.0 76.8 all-gather.1

commit v4 on v2

--- a/solution.py
+++ b/solution.py
@@ -12,12 +12,27 @@
 ALL = FSDP + DP
 
 
-def gather_weight(w):
+def gather_over_fsdp(w):
     n_y = lax.axis_size("y")
     copies = jnp.broadcast_to(w[None], (n_y,) + w.shape).reshape(n_y * w.shape[0], w.shape[1])
     w = lax.all_to_all(copies, "y", 0, 0, tiled=True)
     w = lax.all_gather(w, "xl", axis=0, tiled=True)
     return lax.all_gather(w, "z", axis=0, tiled=True)
+
+
+def swap_join(mine, axis_name):
+    other = lax.ppermute(mine, axis_name, [(0, 1), (1, 0)])
+    first = lax.axis_index(axis_name) == 0
+    return jnp.where(
+        first, jnp.concatenate([mine, other], axis=1), jnp.concatenate([other, mine], axis=1)
+    )
+
+
+def gather_weight(w):
+    width = w.shape[1] // 4
+    quarter = lax.axis_index("c") * 2 + lax.axis_index("xh")
+    mine = gather_over_fsdp(lax.dynamic_slice_in_dim(w, quarter * width, width, axis=1))
+    return swap_join(swap_join(mine, "xh"), "c")
 
 
 def sum_all(parts):

time: 212 us -> 223 us (1.052)
  starting transfers between devices: 33.9 us -> 62 us
  blocking collectives: 37.4 us -> 12.4 us
  other arithmetic: 16.5 us -> 31.7 us
  waiting for transfers between devices: 78.9 us -> 68.3 us
  matrix products: 8.82 us -> 13.3 us
    all_to_all x1, waiting for transfers between devices: 39.1 us -> 16.9 us  [per_device(): lax.all_to_all(jnp.concatenate([outgoing, parked], axis=1), FSDP, split_a...]
    all_to_all x1 -> x0, blocking collectives: 20 us -> none  [gather_weight(): w = lax.all_to_all(copies, 'y', 0, 0, tiled=True)]
    ppermute x0 -> x2, starting transfers between devices: none -> 16.3 us  [swap_join(): other = lax.ppermute(mine, axis_name, [(0, 1), (1, 0)])]
    all_gather x1, waiting for transfers between devices: 22.3 us -> 36.9 us  [gather_over_fsdp(): return lax.all_gather(w, 'z', axis=0, tiled=True)]
    all_to_all x1, starting transfers between devices: 6.17 us -> 14.4 us  [sum_all(): lax.all_to_all(jnp.broadcast_to(mine, flat.shape), FSDP, 0, 0, tiled=True)]
    all_to_all x0 -> x1, starting transfers between devices: none -> 7.64 us  [gather_over_fsdp(): w = lax.all_to_all(copies, 'y', 0, 0, tiled=True)]
    all_to_all x1, waiting for transfers between devices: 7.32 us -> 0.01 us  [sum_all(): mine = lax.all_to_all(flat, FSDP, 0, 0, tiled=True).sum(0, keepdims=True)]
    mul x2, other arithmetic: 1.81 us -> 7.43 us  [conv_module(): mixed_vals = values[:, :chan_count] * jax.nn.sigmoid(values[:, chan_count:])]
  transfers between devices with their start and end apart: 4 -> 7, of which waited for: 4 -> 5; matrix products, arithmetic and copies ran while one was open for 12% -> 18% of each run, Pallas kernels for 0% -> 0%
where the time goes in v4:
time: 223 us; the launch traced here: 221 us
  waiting for transfers between devices  68.3 us (31%)
  starting transfers between devices  62 us (28%)
  other arithmetic  31.7 us (14%)
  local copies, waits for them, and re-layouts  19.4 us (9%)
  between operations  14.4 us (6%)
  matrix products  13.3 us (6%)
  blocking collectives  12.4 us (6%)
    all_gather x1, waiting for transfers between devices, gather_over_fsdp(): return lax.all_gather(w, 'z', axis=0, tiled=True)  36.9 us
    all_to_all x1, waiting for transfers between devices, per_device(): lax.all_to_all(jnp.concatenate([outgoing, parked], axis=1), FSDP, split_a...  16.9 us
    ppermute x2, starting transfers between devices, swap_join(): other = lax.ppermute(mine, axis_name, [(0, 1), (1, 0)])  16.3 us
    all_to_all x1, starting transfers between devices, sum_all(): lax.all_to_all(jnp.broadcast_to(mine, flat.shape), FSDP, 0, 0, tiled=True)  14.4 us
    all_to_all x1, starting transfers between devices, sum_all(): mine = lax.all_to_all(flat, FSDP, 0, 0, tiled=True).sum(0, keepdims=True)  13 us
    all_to_all x1, starting transfers between devices, per_device(): lax.all_to_all(jnp.concatenate([outgoing, parked], axis=1), FSDP, split_a...  10.6 us
    psum x2, blocking collectives, sum_all(): mine = lax.psum(lax.psum(mine, 'c'), 'xh')  8.45 us
    all_to_all x1, waiting for transfers between devices, sum_all(): lax.all_to_all(jnp.broadcast_to(mine, flat.shape), FSDP, 0, 0, tiled=True)  8.3 us
  transfers between devices with their start and end apart: 7, of which 5 were waited for; matrix products, arithmetic and copies ran while one was open for 18% of the time, Pallas kernels for 0%

profile of v4, /device:TPU:1, one launch (start us, length us, event | category | flops | bytes accessed | tf_op | source)
XLA Modules:
  0.0 221.5 jit_solution(7381853998000814723)
XLA Ops:
  8.6 7.6 %all-to-all-start.1 = ((bf16[8,12,384]{2,1,0:T(8,128)(2,1)}), bf16[8,12,384]{2,1,0:T(8,128)(2,1)S(1)}, u32[]{:S(2)}, u32[]{:S(2)}) async-start(bf16[8,12,384]{2,1,0:T(8,128)(2,1)} %broadcast_in_dim.108), calls=%async_computation.1 | async-start | bytes 196608 | tf_op jit(solution)/shard_map/all_to_all | solution.py:18
  20.5 3.4 %all-to-all-done.1 = bf16[8,12,384]{2,1,0:T(8,128)(2,1)S(1)} async-done(((bf16[8,12,384]{2,1,0:T(8,128)(2,1)}), bf16[8,12,384]{2,1,0:T(8,128)(2,1)S(1)}, u32[]{:S(2)}, u32[]{:S(2)}) %all-to-all-start.1) | async-done | bytes 73760 | tf_op jit(solution)/shard_map/all_to_all | solution.py:18
  23.9 4.0 %all_gather.6 = bf16[192,384]{1,0:T(8,128)(2,1)} all-gather(bf16[96,384]{1,0:T(8,128)(2,1)S(1)} %all_to_all.28), channel_id=1, replica_groups=mesh['z'=8,'xl'=2,'y'=8,'xh'=2,'c'=2] {'xl'}, dimensions={0}, use_global_device_ids=true | all-gather | bytes 221184 | tf_op jit(solution)/shard_map/all_gather | solution.py:19
  31.6 36.9 %all-gather.2.cloned.1.call-done = bf16[1536,384]{1,0:T(8,128)(2,1)} async-done(((bf16[192,384]{1,0:T(8,128)(2,1)}), bf16[1536,384]{1,0:T(8,128)(2,1)}) %all-gather.2.cloned.1.call-update) | async-done | bytes 1179664 | tf_op jit(solution)/shard_map/all_gather | solution.py:20
  68.5 4.6 %collective-permute-start = (bf16[1536,384]{1,0:T(8,128)(2,1)}, bf16[1536,384]{1,0:T(8,128)(2,1)}, u32[]{:S(2)}, u32[]{:S(2)}) collective-permute-start(bf16[1536,384]{1,0:T(8,128)(2,1)} %all-gather.2.cloned.1.call-done), channel_id=1, source_target_pairs={{0,2},{2,0},{1,3},{3,1},{4,6},{6,4},{5,7},{7,5},{8,10},{10,8},{9,1... | collective-permute-start | bytes 3538952 | tf_op jit(solution)/shard_map/ppermute | solution.py:24
  73.2 2.8 %scatter_custom_fusion = bf16[256,1536]{1,0:T(8,128)(2,1)} fusion(s32[160]{0:T(256)S(1)} %bitcast.15, bf16[160,1536]{1,0:T(8,128)(2,1)} %param.17, bf16[]{:T(256)} %constant.51.clone.1), kind=kCustom, calls=%fused_computation.55 | custom fusion | bytes 786944 | tf_op jit(solution)/shard_map/scatter | solution.py:100
  76.0 2.1 gather_fusion
  81.2 10.6 %all-to-all-start = ((bf16[128,2,3072]{2,1,0:T(2,128)(2,1)}), bf16[128,2,3072]{2,1,0:T(2,128)(2,1)S(1)}, u32[]{:S(2)}, u32[]{:S(2)}) async-start(bf16[128,2,3072]{2,1,0:T(2,128)(2,1)} %all_to_all.24), calls=%async_computation | async-start | bytes 3145728 | tf_op jit(solution)/shard_map/all_to_all | solution.py:101
  91.8 2.8 %collective-permute-done = bf16[1536,384]{1,0:T(8,128)(2,1)} collective-permute-done((bf16[1536,384]{1,0:T(8,128)(2,1)}, bf16[1536,384]{1,0:T(8,128)(2,1)}, u32[]{:S(2)}, u32[]{:S(2)}) %collective-permute-start) | collective-permute-done | bytes 1179680 | tf_op jit(solution)/shard_map/ppermute | solution.py:24
  94.7 4.0 %maximum_select_fusion.1 = bf16[1536,768]{1,0:T(8,128)(2,1)} fusion(bf16[1536,384]{1,0:T(8,128)(2,1)} %collective-permute-done, bf16[1536,384]{1,0:T(8,128)(2,1)} %all-gather.2.cloned.1.call-done, pred[]{:T(512)S(6)} %eq.24), kind=kLoop, calls=%fused_computation.12 | loop fusion | flops 10616832 | bytes 4718593 | tf_op jit(solution)/shard_map/jit(_where)/select_n | solution.py:26
  98.6 11.7 %collective-permute-start.1 = (bf16[1536,768]{1,0:T(8,128)(2,1)}, bf16[1536,768]{1,0:T(8,128)(2,1)}, u32[]{:S(2)}, u32[]{:S(2)}) collective-permute-start(bf16[1536,768]{1,0:T(8,128)(2,1)} %maximum_select_fusion.1), channel_id=1, source_target_pairs={{0,1},{1,0},{2,3},{3,2},{4,5},{5,4},{6,7},{7,6},{8,9},{9,8},{10,11... | collective-permute-start | bytes 7077896 | tf_op jit(solution)/shard_map/ppermute | solution.py:24
  110.4 16.9 %all-to-all-done = bf16[128,2,3072]{2,1,0:T(2,128)(2,1)S(1)} async-done(((bf16[128,2,3072]{2,1,0:T(2,128)(2,1)}), bf16[128,2,3072]{2,1,0:T(2,128)(2,1)S(1)}, u32[]{:S(2)}, u32[]{:S(2)}) %all-to-all-start) | async-done | bytes 1572896 | tf_op jit(solution)/shard_map/all_to_all | solution.py:101
  129.9 2.8 %scatter_custom_fusion.1 = bf16[257,1536]{1,0:T(8,128)(2,1)S(1)} fusion(s32[256]{0:T(256)S(1)} %bitcast.14, bf16[256,3072]{1,0:T(8,128)(2,1)} %all_to_all.26, bf16[]{:T(256)} %constant.51.clone.1), kind=kCustom, calls=%fused_computation.51 | custom fusion | bytes 1576448 | tf_op jit(solution)/shard_map/scatter | solution.py:110
  134.5 6.7 %multiply_reduce_fusion = (f32[1536]{0:T(1024)S(1)}, f32[256]{0:T(256)S(1)}, f32[256]{0:T(256)S(1)}, f32[1536]{0:T(1024)S(1)}, f32[256,1536]{1,0:T(8,128)S(1)}) fusion(f32[256,1536]{1,0:T(8,128)S(1)} %get-tuple-element.22, f32[256]{0:T(256)S(1)} %fusion.19, f32[256]{0:T(256)S(1)} %broadcast_multiply_fusion.1, f32[1536]{0:T(1024)S(1)} %copy-done.6, ...), kind=kOutput, calls=%fused_computation.26 | convolution fusion | flops 1238626816 | bytes 8684033 | tf_op jit(solution)/shard_map/dot_general | solution.py:112
  142.6 2.4 %multiply_reduce_fusion.5 = (f32[1536]{0:T(1024)S(1)}, f32[1536]{0:T(1024)S(1)}, f32[1536]{0:T(1024)S(1)}, f32[1536]{0:T(1024)S(1)}, f32[1536]{0:T(1024)S(1)}, /*index=5*/f32[256,1536]{1,0:T(8,128)S(1)}) fusion(f32[256,1536]{1,0:T(8,128)S(1)} %copy-done.4, pred[256]{0:T(512)(128)(4,1)S(1)} %get-tuple-element.31, pred[256]{0:T(512)(128)(4,1)S(1)} %get-tuple-element.28, ...), kind=kLoop, calls=%fused_computation.31 | loop fusion | flops 7856640 | bytes 6333440 | tf_op jit(solution)/shard_map/transpose(jvp())/reduce_sum | solution.py:65
  145.0 3.9 %multiply_select_fusion.3 = (f32[256,1536]{1,0:T(8,128)}, f32[256,1536]{1,0:T(8,128)}, f32[256,1536]{1,0:T(8,128)}, f32[256,1536]{1,0:T(8,128)}, f32[256,1536]{1,0:T(8,128)}) fusion(f32[256,1536]{1,0:T(8,128)S(1)} %get-tuple-element.18, f32[1536]{0:T(1024)S(1)} %get-tuple-element.16, pred[256]{0:T(512)(128)(4,1)S(1)} %get-tuple-element.31, ...), kind=kLoop, calls=%fused_computation.35 | loop fusion | flops 3538944 | bytes 9468928 | tf_op jit(solution)/shard_map/transpose(jvp(jit(_where)))/select_n | solution.py:65
  149.8 13.0 %all-to-all-start.2 = ((f32[128,1,84]{2,1,0:T(1,128)}), f32[128,1,84]{2,1,0:T(1,128)S(1)}, u32[]{:S(2)}, u32[]{:S(2)}) async-start(f32[128,1,84]{2,1,0:T(1,128)} %bitcast.7), calls=%async_computation.2 | async-start | bytes 131072 | tf_op jit(solution)/shard_map/all_to_all | solution.py:41
  162.9 5.9 %fusion.4 = (f32[256,1536]{1,0:T(8,128)}, f32[256,1536]{1,0:T(8,128)S(1)}) fusion(f32[256,3072]{1,0:T(8,128)S(1)} %copy-done.2, f32[256,1536]{1,0:T(8,128)} %get-tuple-element.24, f32[256,1536]{1,0:T(8,128)} %get-tuple-element.25, f32[256,1536]{1,0:T(8,128)} %get-tuple-element.26, f32[256,1536]{1,0:T(8,128)} %get-tuple-element.27, ...), kind=kLoop, calls=%fused_computation.15 | loop fusion | flops 4718592 | bytes 14156032 | tf_op jit(solution)/shard_map/transpose(jvp())/mul | solution.py:52
  168.7 6.5 %convolution_convert_fusion.1 = bf16[160,1536]{1,0:T(8,128)(2,1)} fusion(bf16[160,1536]{1,0:T(8,128)(2,1)S(1)} %copy-done.5, bf16[1536,768]{1,0:T(8,128)(2,1)} %collective-permute-done.1, bf16[1536,768]{1,0:T(8,128)(2,1)} %maximum_select_fusion.1, pred[]{:T(512)S(6)} %eq.23), kind=kOutput, calls=%fused_computation.9 | convolution fusion | flops 776454144 | bytes 5701633 | tf_op jit(solution)/shard_map/dot_general | solution.py:106
  177.0 3.2 %psum.16 = f32[1,84]{1,0:T(1,128)S(1)} all-reduce(f32[1,84]{1,0:T(1,128)S(1)} %bitcast.17), channel_id=1, replica_groups=mesh['z'=8,'xl'=2,'y'=8,'xh'=2,'c'=2] {'c'}, use_global_device_ids=true, to_apply=%region_17.18 | all-reduce | flops 84 | bytes 672 | tf_op jit(solution)/shard_map/psum | solution.py:42
  180.1 5.3 %psum.18 = f32[84]{0:T(128)S(1)} all-reduce(f32[84]{0:T(128)S(1)} %bitcast.20), channel_id=1, replica_groups=mesh['z'=8,'xl'=2,'y'=8,'xh'=2,'c'=2] {'xh'}, use_global_device_ids=true, to_apply=%region_18.19 | all-reduce | flops 84 | bytes 672 | tf_op jit(solution)/shard_map/psum | solution.py:42
  186.1 14.4 %all-to-all-start.3 = ((f32[128,1,84]{2,1,0:T(1,128)}), f32[128,1,84]{2,1,0:T(1,128)S(1)}, u32[]{:S(2)}, u32[]{:S(2)}) async-start(f32[128,1,84]{2,1,0:T(1,128)} %broadcast_in_dim.112), calls=%async_computation.3 | async-start | bytes 131072 | tf_op jit(solution)/shard_map/all_to_all | solution.py:43
  200.4 3.2 %add_convert_fusion = bf16[256,3072]{1,0:T(8,128)(2,1)} fusion(f32[256,1536]{1,0:T(8,128)} %fusion.22, f32[256,1536]{1,0:T(8,128)} %get-tuple-element.19), kind=kLoop, calls=%fused_computation.5 | loop fusion | flops 1572864 | bytes 4718592 | tf_op jit(solution)/shard_map/transpose(jvp())/convert_element_type | solution.py:51
  203.7 8.3 %all-to-all-done.3 = f32[128,1,84]{2,1,0:T(1,128)S(1)} async-done(((f32[128,1,84]{2,1,0:T(1,128)}), f32[128,1,84]{2,1,0:T(1,128)S(1)}, u32[]{:S(2)}, u32[]{:S(2)}) %all-to-all-start.3) | async-done | bytes 43040 | tf_op jit(solution)/shard_map/all_to_all | solution.py:43
  (73 shorter events, 24.1 us)
Async XLA Ops:
  7.2 0.8 copy-start
  8.6 15.2 %all-to-all-start.1 = ((bf16[8,12,384]{2,1,0:T(8,128)(2,1)}), bf16[8,12,384]{2,1,0:T(8,128)(2,1)S(1)}, u32[]{:S(2)}, u32[]{:S(2)}) async-start(bf16[8,12,384]{2,1,0:T(8,128)(2,1)} %broadcast_in_dim.108), calls=%async_computation.1 | async-start | bytes 196608 | tf_op jit(solution)/shard_map/all_to_all | solution.py:18
  16.3 52.3 %all-gather.2.cloned.1.call-start = ((), (), s32[]{:S(2)}) async-start(), calls=%async_computation.4 | async-start | bytes 1327104 | tf_op jit(solution)/shard_map/all_gather | solution.py:20
  18.5 1.8 copy-start.7
  20.4 8.0 %copy-start.1 = (f32[256,3072]{1,0:T(8,128)}, f32[256,3072]{1,0:T(8,128)S(1)}, u32[]{:S(2)}) copy-start(f32[256,3072]{1,0:T(8,128)S(1)} %convert_element_type.24) | copy-start | bytes 9437188
  28.3 1.7 copy-start.3
  30.0 0.7 copy-start.6
  30.1 0.7 copy-start.8
  30.4 42.8 %copy-start.9 = (s32[1,160]{1,0:T(1,128)S(1)}, s32[1,160]{1,0:T(1,128)}, u32[]{:S(2)}) copy-start(s32[1,160]{1,0:T(1,128)} %param.12) | copy-start | bytes 1924
  31.6 44.4 %copy-start.10 = (s32[1,256]{1,0:T(1,128)S(1)}, s32[1,256]{1,0:T(1,128)}, u32[]{:S(2)}) copy-start(s32[1,256]{1,0:T(1,128)} %param.11) | copy-start | bytes 3076
  68.5 26.1 %collective-permute-start = (bf16[1536,384]{1,0:T(8,128)(2,1)}, bf16[1536,384]{1,0:T(8,128)(2,1)}, u32[]{:S(2)}, u32[]{:S(2)}) collective-permute-start(bf16[1536,384]{1,0:T(8,128)(2,1)} %all-gather.2.cloned.1.call-done), channel_id=1, source_target_pairs={{0,2},{2,0},{1,3},{3,1},{4,6},{6,4},{5,7},{7,5},{8,10},{10,8},{9,1... | collective-permute-start | bytes 3538952 | tf_op jit(solution)/shard_map/ppermute | solution.py:24
  81.2 46.1 %all-to-all-start = ((bf16[128,2,3072]{2,1,0:T(2,128)(2,1)}), bf16[128,2,3072]{2,1,0:T(2,128)(2,1)S(1)}, u32[]{:S(2)}, u32[]{:S(2)}) async-start(bf16[128,2,3072]{2,1,0:T(2,128)(2,1)} %all_to_all.24), calls=%async_computation | async-start | bytes 3145728 | tf_op jit(solution)/shard_map/all_to_all | solution.py:101
  98.6 35.9 %collective-permute-start.1 = (bf16[1536,768]{1,0:T(8,128)(2,1)}, bf16[1536,768]{1,0:T(8,128)(2,1)}, u32[]{:S(2)}, u32[]{:S(2)}) collective-permute-start(bf16[1536,768]{1,0:T(8,128)(2,1)} %maximum_select_fusion.1), channel_id=1, source_target_pairs={{0,1},{1,0},{2,3},{3,2},{4,5},{5,4},{6,7},{7,6},{8,9},{9,8},{10,11... | collective-permute-start | bytes 7077896 | tf_op jit(solution)/shard_map/ppermute | solution.py:24
  141.2 1.4 copy-start.4
  145.0 17.8 %copy-start.2 = (f32[256,3072]{1,0:T(8,128)S(1)}, f32[256,3072]{1,0:T(8,128)}, u32[]{:S(2)}) copy-start(f32[256,3072]{1,0:T(8,128)} %copy-done.1) | copy-start | bytes 9437188
  149.8 27.0 %all-to-all-start.2 = ((f32[128,1,84]{2,1,0:T(1,128)}), f32[128,1,84]{2,1,0:T(1,128)S(1)}, u32[]{:S(2)}, u32[]{:S(2)}) async-start(f32[128,1,84]{2,1,0:T(1,128)} %bitcast.7), calls=%async_computation.2 | async-start | bytes 131072 | tf_op jit(solution)/shard_map/all_to_all | solution.py:41
  162.8 5.9 %copy-start.5 = (bf16[160,1536]{1,0:T(8,128)(2,1)S(1)}, bf16[160,1536]{1,0:T(8,128)(2,1)}, u32[]{:S(2)}) copy-start(bf16[160,1536]{1,0:T(8,128)(2,1)} %gather_fusion.1) | copy-start | bytes 1474564
  186.1 25.9 %all-to-all-start.3 = ((f32[128,1,84]{2,1,0:T(1,128)}), f32[128,1,84]{2,1,0:T(1,128)S(1)}, u32[]{:S(2)}, u32[]{:S(2)}) async-start(f32[128,1,84]{2,1,0:T(1,128)} %broadcast_in_dim.112), calls=%async_computation.3 | async-start | bytes 131072 | tf_op jit(solution)/shard_map/all_to_all | solution.py:43
Sparse Core Ops, SparseCore 0:
  28.0 40.5 all-gather.1

commit v5 on v4

--- a/solution.py
+++ b/solution.py
@@ -28,10 +28,13 @@
     )
 
 
-def gather_weight(w):
+def fetch_quarter(w):
     width = w.shape[1] // 4
     quarter = lax.axis_index("c") * 2 + lax.axis_index("xh")
-    mine = gather_over_fsdp(lax.dynamic_slice_in_dim(w, quarter * width, width, axis=1))
+    return gather_over_fsdp(lax.dynamic_slice_in_dim(w, quarter * width, width, axis=1))
+
+
+def join_quarters(mine):
     return swap_join(swap_join(mine, "xh"), "c")
 
 
@@ -101,8 +104,9 @@
     moved = lax.all_to_all(
         jnp.concatenate([outgoing, parked], axis=1), FSDP, split_axis=0, concat_axis=0, tiled=True
     )
+    quarter_weight, moved = lax.optimization_barrier((fetch_quarter(point_weight), moved))
     arrived, returned = moved[:, :out_count], moved[:, out_count:]
-    full_weight = gather_weight(point_weight)
+    full_weight = join_quarters(quarter_weight)
     output = jnp.dot(
         arrived[owner_slot], full_weight, preferred_element_type=jnp.float32
     ).astype(jnp.bfloat16)

time: 223 us -> 238 us (1.067)
  waiting for transfers between devices: 68.3 us -> 78.4 us
  starting transfers between devices: 62 us -> 65.6 us
    all_gather x1, waiting for transfers between devices: 36.9 us -> 12.8 us  [gather_over_fsdp(): return lax.all_gather(w, 'z', axis=0, tiled=True)]
    all_to_all x1, waiting for transfers between devices: 16.9 us -> 35.7 us  [per_device(): lax.all_to_all(jnp.concatenate([outgoing, parked], axis=1), FSDP, split_a...]
    ppermute x2, waiting for transfers between devices: 2.84 us -> 21.5 us  [swap_join(): other = lax.ppermute(mine, axis_name, [(0, 1), (1, 0)])]
    all_to_all x1, starting transfers between devices: 10.6 us -> 18.3 us  [per_device(): lax.all_to_all(jnp.concatenate([outgoing, parked], axis=1), FSDP, split_a...]
    ppermute x2, starting transfers between devices: 16.3 us -> 12.4 us  [swap_join(): other = lax.ppermute(mine, axis_name, [(0, 1), (1, 0)])]
    all_to_all x1, waiting for transfers between devices: 3.39 us -> 0.01 us  [gather_over_fsdp(): w = lax.all_to_all(copies, 'y', 0, 0, tiled=True)]
  transfers between devices with their start and end apart: 7 -> 7, of which waited for: 5 -> 4; matrix products, arithmetic and copies ran while one was open for 18% -> 16% of each run, Pallas kernels for 0% -> 0%
where the time goes in v5:
time: 238 us; the launch traced here: 236 us
  waiting for transfers between devices  78.4 us (33%)
  starting transfers between devices  65.6 us (28%)
  other arithmetic  31.7 us (13%)
  local copies, waits for them, and re-layouts  20.9 us (9%)
  between operations  14.4 us (6%)
  matrix products  13.2 us (6%)
  blocking collectives  12.2 us (5%)
    all_to_all x1, waiting for transfers between devices, per_device(): lax.all_to_all(jnp.concatenate([outgoing, parked], axis=1), FSDP, split_a...  35.7 us
    ppermute x2, waiting for transfers between devices, swap_join(): other = lax.ppermute(mine, axis_name, [(0, 1), (1, 0)])  21.5 us
    all_to_all x1, starting transfers between devices, per_device(): lax.all_to_all(jnp.concatenate([outgoing, parked], axis=1), FSDP, split_a...  18.3 us
    all_to_all x1, starting transfers between devices, sum_all(): lax.all_to_all(jnp.broadcast_to(mine, flat.shape), FSDP, 0, 0, tiled=True)  14.3 us
    all_to_all x1, starting transfers between devices, sum_all(): mine = lax.all_to_all(flat, FSDP, 0, 0, tiled=True).sum(0, keepdims=True)  12.9 us
    all_gather x1, waiting for transfers between devices, gather_over_fsdp(): return lax.all_gather(w, 'z', axis=0, tiled=True)  12.8 us
    ppermute x2, starting transfers between devices, swap_join(): other = lax.ppermute(mine, axis_name, [(0, 1), (1, 0)])  12.4 us
    all_to_all x1, waiting for transfers between devices, sum_all(): lax.all_to_all(jnp.broadcast_to(mine, flat.shape), FSDP, 0, 0, tiled=True)  8.3 us
  transfers between devices with their start and end apart: 7, of which 4 were waited for; matrix products, arithmetic and copies ran while one was open for 16% of the time, Pallas kernels for 0%

profile of v5, /device:TPU:1, one launch (start us, length us, event | category | flops | bytes accessed | tf_op | source)
XLA Modules:
  0.0 236.3 jit_solution(11887437797809238160)
XLA Ops:
  8.6 7.6 %all-to-all-start = ((bf16[8,12,384]{2,1,0:T(8,128)(2,1)}), bf16[8,12,384]{2,1,0:T(8,128)(2,1)S(1)}, u32[]{:S(2)}, u32[]{:S(2)}) async-start(bf16[8,12,384]{2,1,0:T(8,128)(2,1)} %broadcast_in_dim.101), calls=%async_computation | async-start | bytes 196608 | tf_op jit(solution)/shard_map/all_to_all | solution.py:18
  26.4 2.8 %scatter_custom_fusion = bf16[256,1536]{1,0:T(8,128)(2,1)} fusion(s32[160]{0:T(256)S(1)} %bitcast.13, bf16[160,1536]{1,0:T(8,128)(2,1)} %param.17, bf16[]{:T(256)} %constant.55.clone.1), kind=kCustom, calls=%fused_computation.55 | custom fusion | bytes 786944 | tf_op jit(solution)/shard_map/scatter | solution.py:103
  29.2 2.1 gather_fusion
  34.4 18.3 %all-to-all-start.1 = ((bf16[128,2,3072]{2,1,0:T(2,128)(2,1)}), bf16[128,2,3072]{2,1,0:T(2,128)(2,1)S(1)}, u32[]{:S(2)}, u32[]{:S(2)}) async-start(bf16[128,2,3072]{2,1,0:T(2,128)(2,1)} %all_to_all.26), calls=%async_computation.1 | async-start | bytes 3145728 | tf_op jit(solution)/shard_map/all_to_all | solution.py:104
  52.7 4.4 %all_gather.6 = bf16[192,384]{1,0:T(8,128)(2,1)} all-gather(bf16[96,384]{1,0:T(8,128)(2,1)S(1)} %all_to_all.25), channel_id=1, replica_groups=mesh['z'=8,'xl'=2,'y'=8,'xh'=2,'c'=2] {'xl'}, dimensions={0}, use_global_device_ids=true | all-gather | bytes 221184 | tf_op jit(solution)/shard_map/all_gather | solution.py:19
  57.2 35.7 %all-to-all-done.1 = bf16[128,2,3072]{2,1,0:T(2,128)(2,1)S(1)} async-done(((bf16[128,2,3072]{2,1,0:T(2,128)(2,1)}), bf16[128,2,3072]{2,1,0:T(2,128)(2,1)S(1)}, u32[]{:S(2)}, u32[]{:S(2)}) %all-to-all-start.1) | async-done | bytes 1572896 | tf_op jit(solution)/shard_map/all_to_all | solution.py:104
  94.4 12.8 %all-gather.2.cloned.1.call-done = bf16[1536,384]{1,0:T(8,128)(2,1)} async-done(((bf16[192,384]{1,0:T(8,128)(2,1)}), bf16[1536,384]{1,0:T(8,128)(2,1)}) %all-gather.2.cloned.1.call-update) | async-done | bytes 1179664 | tf_op jit(solution)/shard_map/all_gather | solution.py:20
  107.2 4.9 %collective-permute-start = (bf16[1536,384]{1,0:T(8,128)(2,1)}, bf16[1536,384]{1,0:T(8,128)(2,1)S(1)}, u32[]{:S(2)}, u32[]{:S(2)}) collective-permute-start(bf16[1536,384]{1,0:T(8,128)(2,1)} %all-gather.2.cloned.1.call-done), channel_id=1, source_target_pairs={{0,2},{2,0},{1,3},{3,1},{4,6},{6,4},{5,7},{7,5},{8,10},{10,8},{9,1... | collective-permute-start | bytes 3538952 | tf_op jit(solution)/shard_map/ppermute | solution.py:24
  112.2 21.5 %collective-permute-done = bf16[1536,384]{1,0:T(8,128)(2,1)S(1)} collective-permute-done((bf16[1536,384]{1,0:T(8,128)(2,1)}, bf16[1536,384]{1,0:T(8,128)(2,1)S(1)}, u32[]{:S(2)}, u32[]{:S(2)}) %collective-permute-start) | collective-permute-done | bytes 1179680 | tf_op jit(solution)/shard_map/ppermute | solution.py:24
  133.7 3.3 %maximum_select_fusion.1 = bf16[1536,768]{1,0:T(8,128)(2,1)} fusion(bf16[1536,384]{1,0:T(8,128)(2,1)S(1)} %collective-permute-done, bf16[1536,384]{1,0:T(8,128)(2,1)} %all-gather.2.cloned.1.call-done, pred[]{:T(512)S(6)} %eq.24), kind=kLoop, calls=%fused_computation.12 | loop fusion | flops 10616832 | bytes 4718593 | tf_op jit(solution)/shard_map/jit(_where)/select_n | solution.py:26
  137.0 7.5 %collective-permute-start.1 = (bf16[1536,768]{1,0:T(8,128)(2,1)}, bf16[1536,768]{1,0:T(8,128)(2,1)}, u32[]{:S(2)}, u32[]{:S(2)}) collective-permute-start(bf16[1536,768]{1,0:T(8,128)(2,1)} %maximum_select_fusion.1), channel_id=1, source_target_pairs={{0,1},{1,0},{2,3},{3,2},{4,5},{5,4},{6,7},{7,6},{8,9},{9,8},{10,11... | collective-permute-start | bytes 7077896 | tf_op jit(solution)/shard_map/ppermute | solution.py:24
  145.7 2.8 %scatter_custom_fusion.1 = bf16[257,1536]{1,0:T(8,128)(2,1)S(1)} fusion(s32[256]{0:T(256)S(1)} %bitcast.16, bf16[256,3072]{1,0:T(8,128)(2,1)} %all_to_all.28, bf16[]{:T(256)} %constant.55.clone.1), kind=kCustom, calls=%fused_computation.51 | custom fusion | bytes 1576448 | tf_op jit(solution)/shard_map/scatter | solution.py:114
  148.5 1.8 gather_fusion.1
  150.3 6.7 %multiply_reduce_fusion = (f32[1536]{0:T(1024)S(1)}, f32[256]{0:T(256)S(1)}, f32[256]{0:T(256)S(1)}, f32[1536]{0:T(1024)S(1)}, f32[256,1536]{1,0:T(8,128)S(1)}) fusion(f32[256,1536]{1,0:T(8,128)S(1)} %get-tuple-element.26, f32[256]{0:T(256)S(1)} %fusion.19, f32[256]{0:T(256)S(1)} %broadcast_multiply_fusion.1, f32[1536]{0:T(1024)S(1)} %copy-done.6, ...), kind=kOutput, calls=%fused_computation.26 | convolution fusion | flops 1238626816 | bytes 8684033 | tf_op jit(solution)/shard_map/dot_general | solution.py:116
  158.4 2.4 %multiply_reduce_fusion.5 = (f32[1536]{0:T(1024)S(1)}, f32[1536]{0:T(1024)S(1)}, f32[1536]{0:T(1024)S(1)}, f32[1536]{0:T(1024)S(1)}, f32[1536]{0:T(1024)S(1)}, /*index=5*/f32[256,1536]{1,0:T(8,128)S(1)}) fusion(f32[256,1536]{1,0:T(8,128)S(1)} %copy-done.4, pred[256]{0:T(512)(128)(4,1)S(1)} %get-tuple-element.35, pred[256]{0:T(512)(128)(4,1)S(1)} %get-tuple-element.32, ...), kind=kLoop, calls=%fused_computation.31 | loop fusion | flops 7856640 | bytes 6333440 | tf_op jit(solution)/shard_map/transpose(jvp())/reduce_sum | solution.py:68
  160.8 3.9 %multiply_select_fusion.3 = (f32[256,1536]{1,0:T(8,128)}, f32[256,1536]{1,0:T(8,128)}, f32[256,1536]{1,0:T(8,128)}, f32[256,1536]{1,0:T(8,128)}, f32[256,1536]{1,0:T(8,128)}) fusion(f32[256,1536]{1,0:T(8,128)S(1)} %get-tuple-element.22, f32[1536]{0:T(1024)S(1)} %get-tuple-element.20, pred[256]{0:T(512)(128)(4,1)S(1)} %get-tuple-element.35, ...), kind=kLoop, calls=%fused_computation.35 | loop fusion | flops 3538944 | bytes 9468928 | tf_op jit(solution)/shard_map/transpose(jvp(jit(_where)))/select_n | solution.py:68
  165.6 12.9 %all-to-all-start.2 = ((f32[128,1,84]{2,1,0:T(1,128)}), f32[128,1,84]{2,1,0:T(1,128)S(1)}, u32[]{:S(2)}, u32[]{:S(2)}) async-start(f32[128,1,84]{2,1,0:T(1,128)} %bitcast.7), calls=%async_computation.2 | async-start | bytes 131072 | tf_op jit(solution)/shard_map/all_to_all | solution.py:44
  178.5 5.9 %fusion.4 = (f32[256,1536]{1,0:T(8,128)}, f32[256,1536]{1,0:T(8,128)S(1)}) fusion(f32[256,3072]{1,0:T(8,128)S(1)} %copy-done.2, f32[256,1536]{1,0:T(8,128)} %get-tuple-element.28, f32[256,1536]{1,0:T(8,128)} %get-tuple-element.29, f32[256,1536]{1,0:T(8,128)} %get-tuple-element.30, f32[256,1536]{1,0:T(8,128)} %get-tuple-element.31, ...), kind=kLoop, calls=%fused_computation.15 | loop fusion | flops 4718592 | bytes 14156032 | tf_op jit(solution)/shard_map/transpose(jvp())/mul | solution.py:55
  184.4 6.5 %convolution_convert_fusion.1 = bf16[160,1536]{1,0:T(8,128)(2,1)} fusion(bf16[160,1536]{1,0:T(8,128)(2,1)S(1)} %copy-done.5, bf16[1536,768]{1,0:T(8,128)(2,1)} %collective-permute-done.1, bf16[1536,768]{1,0:T(8,128)(2,1)} %maximum_select_fusion.1, pred[]{:T(512)S(6)} %eq.23), kind=kOutput, calls=%fused_computation.9 | convolution fusion | flops 776454144 | bytes 5701633 | tf_op jit(solution)/shard_map/dot_general | solution.py:110
  192.6 2.5 %psum.16 = f32[1,84]{1,0:T(1,128)S(1)} all-reduce(f32[1,84]{1,0:T(1,128)S(1)} %bitcast.17), channel_id=1, replica_groups=mesh['z'=8,'xl'=2,'y'=8,'xh'=2,'c'=2] {'c'}, use_global_device_ids=true, to_apply=%region_17.18 | all-reduce | flops 84 | bytes 672 | tf_op jit(solution)/shard_map/psum | solution.py:45
  195.1 5.3 %psum.18 = f32[84]{0:T(128)S(1)} all-reduce(f32[84]{0:T(128)S(1)} %bitcast.20), channel_id=1, replica_groups=mesh['z'=8,'xl'=2,'y'=8,'xh'=2,'c'=2] {'xh'}, use_global_device_ids=true, to_apply=%region_18.19 | all-reduce | flops 84 | bytes 672 | tf_op jit(solution)/shard_map/psum | solution.py:45
  201.0 14.3 %all-to-all-start.3 = ((f32[128,1,84]{2,1,0:T(1,128)}), f32[128,1,84]{2,1,0:T(1,128)S(1)}, u32[]{:S(2)}, u32[]{:S(2)}) async-start(f32[128,1,84]{2,1,0:T(1,128)} %broadcast_in_dim.112), calls=%async_computation.3 | async-start | bytes 131072 | tf_op jit(solution)/shard_map/all_to_all | solution.py:46
  215.3 3.2 %add_convert_fusion = bf16[256,3072]{1,0:T(8,128)(2,1)} fusion(f32[256,1536]{1,0:T(8,128)} %fusion.22, f32[256,1536]{1,0:T(8,128)} %get-tuple-element.23), kind=kLoop, calls=%fused_computation.5 | loop fusion | flops 1572864 | bytes 4718592 | tf_op jit(solution)/shard_map/transpose(jvp())/convert_element_type | solution.py:54
  218.5 8.3 %all-to-all-done.3 = f32[128,1,84]{2,1,0:T(1,128)S(1)} async-done(((f32[128,1,84]{2,1,0:T(1,128)}), f32[128,1,84]{2,1,0:T(1,128)S(1)}, u32[]{:S(2)}, u32[]{:S(2)}) %all-to-all-start.3) | async-done | bytes 43040 | tf_op jit(solution)/shard_map/all_to_all | solution.py:46
  (69 shorter events, 24.5 us)
Async XLA Ops:
  7.2 0.8 copy-start
  8.6 25.8 %all-to-all-start = ((bf16[8,12,384]{2,1,0:T(8,128)(2,1)}), bf16[8,12,384]{2,1,0:T(8,128)(2,1)S(1)}, u32[]{:S(2)}, u32[]{:S(2)}) async-start(bf16[8,12,384]{2,1,0:T(8,128)(2,1)} %broadcast_in_dim.101), calls=%async_computation | async-start | bytes 196608 | tf_op jit(solution)/shard_map/all_to_all | solution.py:18
  21.4 1.7 copy-start.1
  23.1 1.7 copy-start.3
  24.8 0.7 copy-start.8
  24.8 0.7 copy-start.6
  24.8 0.7 copy-start.7
  34.4 58.5 %all-to-all-start.1 = ((bf16[128,2,3072]{2,1,0:T(2,128)(2,1)}), bf16[128,2,3072]{2,1,0:T(2,128)(2,1)S(1)}, u32[]{:S(2)}, u32[]{:S(2)}) async-start(bf16[128,2,3072]{2,1,0:T(2,128)(2,1)} %all_to_all.26), calls=%async_computation.1 | async-start | bytes 3145728 | tf_op jit(solution)/shard_map/all_to_all | solution.py:104
  52.7 54.5 %all-gather.2.cloned.1.call-start = ((), (), s32[]{:S(2)}) async-start(), calls=%async_computation.4 | async-start | bytes 1327104 | tf_op jit(solution)/shard_map/all_gather | solution.py:20
  107.2 26.5 %collective-permute-start = (bf16[1536,384]{1,0:T(8,128)(2,1)}, bf16[1536,384]{1,0:T(8,128)(2,1)S(1)}, u32[]{:S(2)}, u32[]{:S(2)}) collective-permute-start(bf16[1536,384]{1,0:T(8,128)(2,1)} %all-gather.2.cloned.1.call-done), channel_id=1, source_target_pairs={{0,2},{2,0},{1,3},{3,1},{4,6},{6,4},{5,7},{7,5},{8,10},{10,8},{9,1... | collective-permute-start | bytes 3538952 | tf_op jit(solution)/shard_map/ppermute | solution.py:24
  137.0 13.2 %collective-permute-start.1 = (bf16[1536,768]{1,0:T(8,128)(2,1)}, bf16[1536,768]{1,0:T(8,128)(2,1)}, u32[]{:S(2)}, u32[]{:S(2)}) collective-permute-start(bf16[1536,768]{1,0:T(8,128)(2,1)} %maximum_select_fusion.1), channel_id=1, source_target_pairs={{0,1},{1,0},{2,3},{3,2},{4,5},{5,4},{6,7},{7,6},{8,9},{9,8},{10,11... | collective-permute-start | bytes 7077896 | tf_op jit(solution)/shard_map/ppermute | solution.py:24
  157.0 1.4 copy-start.4
  160.8 17.7 %copy-start.2 = (f32[256,3072]{1,0:T(8,128)S(1)}, f32[256,3072]{1,0:T(8,128)}, u32[]{:S(2)}) copy-start(f32[256,3072]{1,0:T(8,128)} %copy-done.1) | copy-start | bytes 9437188
  165.6 26.8 %all-to-all-start.2 = ((f32[128,1,84]{2,1,0:T(1,128)}), f32[128,1,84]{2,1,0:T(1,128)S(1)}, u32[]{:S(2)}, u32[]{:S(2)}) async-start(f32[128,1,84]{2,1,0:T(1,128)} %bitcast.7), calls=%async_computation.2 | async-start | bytes 131072 | tf_op jit(solution)/shard_map/all_to_all | solution.py:44
  178.5 5.9 %copy-start.5 = (bf16[160,1536]{1,0:T(8,128)(2,1)S(1)}, bf16[160,1536]{1,0:T(8,128)(2,1)}, u32[]{:S(2)}) copy-start(bf16[160,1536]{1,0:T(8,128)(2,1)} %gather_fusion.1) | copy-start | bytes 1474564
  201.0 25.8 %all-to-all-start.3 = ((f32[128,1,84]{2,1,0:T(1,128)}), f32[128,1,84]{2,1,0:T(1,128)S(1)}, u32[]{:S(2)}, u32[]{:S(2)}) async-start(f32[128,1,84]{2,1,0:T(1,128)} %broadcast_in_dim.112), calls=%async_computation.3 | async-start | bytes 131072 | tf_op jit(solution)/shard_map/all_to_all | solution.py:46
Sparse Core Ops, SparseCore 0:
  57.3 49.8 all-gather.1

commit v6 on v3

--- a/solution.py
+++ b/solution.py
@@ -31,11 +31,10 @@
 
 
 def sum_all(parts):
-    n_f = lax.axis_size(FSDP)
-    flat = parts.reshape(n_f, -1)
-    mine = lax.all_to_all(flat, FSDP, 0, 0, tiled=True).sum(0, keepdims=True)
-    mine = lax.psum(lax.psum(mine, "c"), "xh")
-    whole = lax.all_to_all(jnp.broadcast_to(mine, flat.shape), FSDP, 0, 0, tiled=True)
+    n_all = lax.axis_size(ALL)
+    flat = parts.reshape(n_all, -1)
+    mine = lax.all_to_all(flat, ALL, 0, 0, tiled=True).sum(0, keepdims=True)
+    whole = lax.all_to_all(jnp.broadcast_to(mine, flat.shape), ALL, 0, 0, tiled=True)
     return whole.reshape(parts.shape)
 
 

time: 207 us -> 212 us (1.024)
  waiting for transfers between devices: 60.2 us -> 69.7 us
  blocking collectives: 12.5 us -> 4.76 us
  starting transfers between devices: 55.2 us -> 58.9 us
    all_to_all x2, waiting for transfers between devices: 8.3 us -> 17.7 us  [the longest x1 13.8 us: sum_all(): lax.all_to_all(jnp.broadcast_to(mine, flat.shape), ALL, 0, 0, tiled=True)]
    psum x2 -> x0, blocking collectives: 7.73 us -> none  [sum_all(): mine = lax.psum(lax.psum(mine, 'c'), 'xh')]
    all_to_all x2, starting transfers between devices: 26.2 us -> 30 us  [the longest x1 15.4 us: sum_all(): lax.all_to_all(jnp.broadcast_to(mine, flat.shape), ALL, 0, 0, tiled=True)]
  transfers between devices with their start and end apart: 6 -> 6, of which waited for: 3 -> 4; matrix products, arithmetic and copies ran while one was open for 19% -> 18% of each run, Pallas kernels for 0% -> 0%
where the time goes in v6:
time: 212 us; the launch traced here: 211 us
  waiting for transfers between devices  69.7 us (33%)
  starting transfers between devices  58.9 us (28%)
  other arithmetic  30.3 us (14%)
  local copies, waits for them, and re-layouts  21 us (10%)
  between operations  14.4 us (7%)
  matrix products  12.2 us (6%)
  blocking collectives  4.76 us (2%)
    all_gather x1, waiting for transfers between devices, gather_over_fsdp(): return lax.all_gather(w, 'z', axis=0, tiled=True)  48.1 us
    all_to_all x1, starting transfers between devices, sum_all(): lax.all_to_all(jnp.broadcast_to(mine, flat.shape), ALL, 0, 0, tiled=True)  15.4 us
    all_to_all x1, starting transfers between devices, per_device(): lax.all_to_all(jnp.concatenate([outgoing, parked], axis=1), FSDP, split_a...  15.2 us
    all_to_all x1, starting transfers between devices, sum_all(): mine = lax.all_to_all(flat, ALL, 0, 0, tiled=True).sum(0, keepdims=True)  14.6 us
    all_to_all x1, waiting for transfers between devices, sum_all(): lax.all_to_all(jnp.broadcast_to(mine, flat.shape), ALL, 0, 0, tiled=True)  13.8 us
    all_to_all x1, starting transfers between devices, gather_over_fsdp(): w = lax.all_to_all(copies, 'y', 0, 0, tiled=True)  7.64 us
    mul x2, other arithmetic, conv_module(): mixed_vals = values[:, :chan_count] * jax.nn.sigmoid(values[:, chan_count:])  7.53 us
    dot_general x1, matrix products, per_device(): lax.dot_general(home_rows, full_weight, (((1,), (1,)), ((), ())), preferr...  6.74 us
  transfers between devices with their start and end apart: 6, of which 4 were waited for; matrix products, arithmetic and copies ran while one was open for 18% of the time, Pallas kernels for 0%

profile of v6, /device:TPU:1, one launch (start us, length us, event | category | flops | bytes accessed | tf_op | source)
XLA Modules:
  0.0 211.2 jit_solution(16995717143216638464)
XLA Ops:
  8.7 7.6 %all-to-all-start.1 = ((bf16[8,12,768]{2,1,0:T(8,128)(2,1)}), bf16[8,12,768]{2,1,0:T(8,128)(2,1)S(1)}, u32[]{:S(2)}, u32[]{:S(2)}) async-start(bf16[8,12,768]{2,1,0:T(8,128)(2,1)} %broadcast_in_dim.106), calls=%async_computation.1 | async-start | bytes 393216 | tf_op jit(solution)/shard_map/all_to_all | solution.py:18
  17.2 1.8 convert_element_type.24
  21.2 3.9 %all-to-all-done.1 = bf16[8,12,768]{2,1,0:T(8,128)(2,1)S(1)} async-done(((bf16[8,12,768]{2,1,0:T(8,128)(2,1)}), bf16[8,12,768]{2,1,0:T(8,128)(2,1)S(1)}, u32[]{:S(2)}, u32[]{:S(2)}) %all-to-all-start.1) | async-done | bytes 147488 | tf_op jit(solution)/shard_map/all_to_all | solution.py:18
  25.1 4.8 %all_gather.6 = bf16[192,768]{1,0:T(8,128)(2,1)} all-gather(bf16[96,768]{1,0:T(8,128)(2,1)S(1)} %all_to_all.28), channel_id=1, replica_groups=mesh['z'=8,'xl'=2,'y'=8,'xh'=2,'c'=2] {'xl'}, dimensions={0}, use_global_device_ids=true | all-gather | bytes 442368 | tf_op jit(solution)/shard_map/all_gather | solution.py:19
  32.2 1.7 fusion.24
  35.6 2.8 %scatter_custom_fusion = bf16[256,1536]{1,0:T(8,128)(2,1)} fusion(s32[160]{0:T(256)S(1)} %bitcast.14, bf16[160,1536]{1,0:T(8,128)(2,1)} %param.17, bf16[]{:T(256)} %constant.48.clone.1), kind=kCustom, calls=%fused_computation.54 | custom fusion | bytes 786944 | tf_op jit(solution)/shard_map/scatter | solution.py:94
  38.4 2.2 %gather_fusion = bf16[256,1536]{1,0:T(8,128)(2,1)} fusion(bf16[257,1536]{1,0:T(8,128)(2,1)S(1)} %concatenate.15, s32[1024]{0:T(1024)S(1)} %pad_clamp_fusion.1), kind=kCustom, calls=%fused_computation | custom fusion | bytes 1573888 | tf_op jit(solution)/shard_map/gather | solution.py:91
  40.6 1.5 pad_maximum_fusion
  43.6 15.2 %all-to-all-start = ((bf16[128,2,3072]{2,1,0:T(2,128)(2,1)}), bf16[128,2,3072]{2,1,0:T(2,128)(2,1)S(1)}, u32[]{:S(2)}, u32[]{:S(2)}) async-start(bf16[128,2,3072]{2,1,0:T(2,128)(2,1)} %all_to_all.24), calls=%async_computation | async-start | bytes 3145728 | tf_op jit(solution)/shard_map/all_to_all | solution.py:95
  58.9 48.1 %all-gather.2.cloned.1.call-done = bf16[1536,768]{1,0:T(8,128)(2,1)} async-done(((bf16[192,768]{1,0:T(8,128)(2,1)}), bf16[1536,768]{1,0:T(8,128)(2,1)}) %all-gather.2.cloned.1.call-update) | async-done | bytes 2359312 | tf_op jit(solution)/shard_map/all_gather | solution.py:20
  106.9 6.0 %collective-permute-start = (bf16[1536,768]{1,0:T(8,128)(2,1)}, bf16[1536,768]{1,0:T(8,128)(2,1)}, u32[]{:S(2)}, u32[]{:S(2)}) collective-permute-start(bf16[1536,768]{1,0:T(8,128)(2,1)} %all-gather.2.cloned.1.call-done), channel_id=1, source_target_pairs={{0,1},{1,0},{2,3},{3,2},{4,5},{5,4},{6,7},{7,6},{8,9},{9,8},{10,11... | collective-permute-start | bytes 7077896 | tf_op jit(solution)/shard_map/ppermute | solution.py:27
  115.7 2.8 %scatter_custom_fusion.1 = bf16[257,1536]{1,0:T(8,128)(2,1)S(1)} fusion(s32[256]{0:T(256)S(1)} %bitcast.13, bf16[256,3072]{1,0:T(8,128)(2,1)} %all_to_all.26, bf16[]{:T(256)} %constant.48.clone.1), kind=kCustom, calls=%fused_computation.50 | custom fusion | bytes 1576448 | tf_op jit(solution)/shard_map/scatter | solution.py:104
  118.5 1.8 gather_fusion.1
  120.2 6.7 %multiply_reduce_fusion = (f32[1536]{0:T(1024)S(1)}, f32[256]{0:T(256)S(1)}, f32[256]{0:T(256)S(1)}, f32[1536]{0:T(1024)S(1)}, f32[256,1536]{1,0:T(8,128)S(1)}) fusion(f32[256,1536]{1,0:T(8,128)S(1)} %get-tuple-element.22, f32[256]{0:T(256)S(1)} %fusion.19, f32[256]{0:T(256)S(1)} %broadcast_multiply_fusion.1, f32[1536]{0:T(1024)S(1)} %copy-done.9, ...), kind=kOutput, calls=%fused_computation.25 | convolution fusion | flops 1238626816 | bytes 8684033 | tf_op jit(solution)/shard_map/dot_general | solution.py:106
  128.4 2.4 %multiply_reduce_fusion.5 = (f32[1536]{0:T(1024)S(1)}, f32[1536]{0:T(1024)S(1)}, f32[1536]{0:T(1024)S(1)}, f32[1536]{0:T(1024)S(1)}, f32[1536]{0:T(1024)S(1)}, /*index=5*/f32[256,1536]{1,0:T(8,128)S(1)}) fusion(f32[256,1536]{1,0:T(8,128)S(1)} %copy-done.4, pred[256]{0:T(512)(128)(4,1)S(1)} %get-tuple-element.31, pred[256]{0:T(512)(128)(4,1)S(1)} %get-tuple-element.28, ...), kind=kLoop, calls=%fused_computation.30 | loop fusion | flops 7856640 | bytes 6333440 | tf_op jit(solution)/shard_map/transpose(jvp())/reduce_sum | solution.py:59
  130.8 3.9 %multiply_select_fusion.3 = (f32[256,1536]{1,0:T(8,128)}, f32[256,1536]{1,0:T(8,128)}, f32[256,1536]{1,0:T(8,128)}, f32[256,1536]{1,0:T(8,128)}, f32[256,1536]{1,0:T(8,128)}) fusion(f32[256,1536]{1,0:T(8,128)S(1)} %get-tuple-element.18, f32[1536]{0:T(1024)S(1)} %copy-done.7, pred[256]{0:T(512)(128)(4,1)S(1)} %get-tuple-element.31, ...), kind=kLoop, calls=%fused_computation.34 | loop fusion | flops 3538944 | bytes 9468928 | tf_op jit(solution)/shard_map/transpose(jvp(jit(_where)))/select_n | solution.py:59
  135.8 14.6 %all-to-all-start.2 = ((f32[512,1,21]{2,1,0:T(1,128)}), f32[512,1,21]{2,1,0:T(1,128)S(1)}, u32[]{:S(2)}, u32[]{:S(2)}) async-start(f32[512,1,21]{2,1,0:T(1,128)} %bitcast.11), calls=%async_computation.2 | async-start | bytes 524288 | tf_op jit(solution)/shard_map/all_to_all | solution.py:36
  150.4 6.0 %fusion.4 = (f32[256,1536]{1,0:T(8,128)}, f32[256,1536]{1,0:T(8,128)S(1)}) fusion(f32[256,3072]{1,0:T(8,128)S(1)} %copy-done.2, f32[256,1536]{1,0:T(8,128)} %get-tuple-element.24, f32[256,1536]{1,0:T(8,128)} %get-tuple-element.25, f32[256,1536]{1,0:T(8,128)} %get-tuple-element.26, f32[256,1536]{1,0:T(8,128)} %get-tuple-element.27, ...), kind=kLoop, calls=%fused_computation.14 | loop fusion | flops 4718592 | bytes 14156032 | tf_op jit(solution)/shard_map/transpose(jvp())/mul | solution.py:46
  156.3 5.4 %convolution_convert_fusion.1 = bf16[160,1536]{1,0:T(8,128)(2,1)} fusion(bf16[160,1536]{1,0:T(8,128)(2,1)S(1)} %copy-done.5, bf16[1536,768]{1,0:T(8,128)(2,1)} %collective-permute-done, bf16[1536,768]{1,0:T(8,128)(2,1)S(1)} %copy-done.14, pred[]{:T(512)S(6)} %eq.20), kind=kOutput, calls=%fused_computation.9 | convolution fusion | flops 776454144 | bytes 5701633 | tf_op jit(solution)/shard_map/dot_general | solution.py:100
  161.8 1.6 fusion.22
  163.3 4.0 %all-to-all-done.2 = f32[512,1,21]{2,1,0:T(1,128)S(1)} async-done(((f32[512,1,21]{2,1,0:T(1,128)}), f32[512,1,21]{2,1,0:T(1,128)S(1)}, u32[]{:S(2)}, u32[]{:S(2)}) %all-to-all-start.2) | async-done | bytes 43040 | tf_op jit(solution)/shard_map/all_to_all | solution.py:36
  168.7 15.4 %all-to-all-start.3 = ((f32[512,1,21]{2,1,0:T(1,128)}), f32[512,1,21]{2,1,0:T(1,128)S(1)}, u32[]{:S(2)}, u32[]{:S(2)}) async-start(f32[512,1,21]{2,1,0:T(1,128)} %broadcast_in_dim.109), calls=%async_computation.3 | async-start | bytes 524288 | tf_op jit(solution)/shard_map/all_to_all | solution.py:37
  184.1 3.2 %add_convert_fusion = bf16[256,3072]{1,0:T(8,128)(2,1)} fusion(f32[256,1536]{1,0:T(8,128)} %fusion.22, f32[256,1536]{1,0:T(8,128)} %get-tuple-element.19), kind=kLoop, calls=%fused_computation.5 | loop fusion | flops 1572864 | bytes 4718592 | tf_op jit(solution)/shard_map/transpose(jvp())/convert_element_type | solution.py:45
  187.3 13.8 %all-to-all-done.3 = f32[512,1,21]{2,1,0:T(1,128)S(1)} async-done(((f32[512,1,21]{2,1,0:T(1,128)}), f32[512,1,21]{2,1,0:T(1,128)S(1)}, u32[]{:S(2)}, u32[]{:S(2)}) %all-to-all-start.3) | async-done | bytes 43040 | tf_op jit(solution)/shard_map/all_to_all | solution.py:37
  (76 shorter events, 19.9 us)
Async XLA Ops:
  7.2 0.8 copy-start
  8.7 16.4 %all-to-all-start.1 = ((bf16[8,12,768]{2,1,0:T(8,128)(2,1)}), bf16[8,12,768]{2,1,0:T(8,128)(2,1)S(1)}, u32[]{:S(2)}, u32[]{:S(2)}) async-start(bf16[8,12,768]{2,1,0:T(8,128)(2,1)} %broadcast_in_dim.106), calls=%async_computation.1 | async-start | bytes 393216 | tf_op jit(solution)/shard_map/all_to_all | solution.py:18
  16.3 90.6 %all-gather.2.cloned.1.call-start = ((), (), s32[]{:S(2)}) async-start(), calls=%async_computation.4 | async-start | bytes 2654208 | tf_op jit(solution)/shard_map/all_gather | solution.py:20
  17.2 3.3 %copy-start.10 = (f32[5,1536]{1,0:T(8,128)S(1)}, f32[5,1536]{1,0:T(8,128)}, u32[]{:S(2)}) copy-start(f32[5,1536]{1,0:T(8,128)} %param.13) | copy-start | bytes 92164
  19.0 13.0 %copy-start.1 = (f32[256,3072]{1,0:T(8,128)}, f32[256,3072]{1,0:T(8,128)S(1)}, u32[]{:S(2)}) copy-start(f32[256,3072]{1,0:T(8,128)S(1)} %convert_element_type.24) | copy-start | bytes 9437188
  31.5 0.7 copy-start.6
  31.5 0.7 copy-start.7
  31.5 0.7 copy-start.8
  31.9 2.0 copy-start.3
  33.9 0.7 copy-start.9
  33.9 0.7 copy-start.11
  34.6 0.9 copy-start.12
  35.5 2.9 %copy-start.13 = (s32[1,256]{1,0:T(1,128)S(1)}, s32[1,256]{1,0:T(1,128)}, u32[]{:S(2)}) copy-start(s32[1,256]{1,0:T(1,128)} %param.11) | copy-start | bytes 3076
  43.6 69.3 %all-to-all-start = ((bf16[128,2,3072]{2,1,0:T(2,128)(2,1)}), bf16[128,2,3072]{2,1,0:T(2,128)(2,1)S(1)}, u32[]{:S(2)}, u32[]{:S(2)}) async-start(bf16[128,2,3072]{2,1,0:T(2,128)(2,1)} %all_to_all.24), calls=%async_computation | async-start | bytes 3145728 | tf_op jit(solution)/shard_map/all_to_all | solution.py:95
  106.9 13.3 %collective-permute-start = (bf16[1536,768]{1,0:T(8,128)(2,1)}, bf16[1536,768]{1,0:T(8,128)(2,1)}, u32[]{:S(2)}, u32[]{:S(2)}) collective-permute-start(bf16[1536,768]{1,0:T(8,128)(2,1)} %all-gather.2.cloned.1.call-done), channel_id=1, source_target_pairs={{0,1},{1,0},{2,3},{3,2},{4,5},{5,4},{6,7},{7,6},{8,9},{9,8},{10,11... | collective-permute-start | bytes 7077896 | tf_op jit(solution)/shard_map/ppermute | solution.py:27
  127.0 1.4 copy-start.4
  130.8 19.6 %copy-start.2 = (f32[256,3072]{1,0:T(8,128)S(1)}, f32[256,3072]{1,0:T(8,128)}, u32[]{:S(2)}) copy-start(f32[256,3072]{1,0:T(8,128)} %copy-done.1) | copy-start | bytes 9437188
  135.8 31.6 %all-to-all-start.2 = ((f32[512,1,21]{2,1,0:T(1,128)}), f32[512,1,21]{2,1,0:T(1,128)S(1)}, u32[]{:S(2)}, u32[]{:S(2)}) async-start(f32[512,1,21]{2,1,0:T(1,128)} %bitcast.11), calls=%async_computation.2 | async-start | bytes 524288 | tf_op jit(solution)/shard_map/all_to_all | solution.py:36
  150.3 6.0 %copy-start.5 = (bf16[160,1536]{1,0:T(8,128)(2,1)S(1)}, bf16[160,1536]{1,0:T(8,128)(2,1)}, u32[]{:S(2)}) copy-start(bf16[160,1536]{1,0:T(8,128)(2,1)} %gather_fusion.1) | copy-start | bytes 1474564
  150.4 6.0 %copy-start.14 = (bf16[1536,768]{1,0:T(8,128)(2,1)S(1)}, bf16[1536,768]{1,0:T(8,128)(2,1)}, u32[]{:S(2)}) copy-start(bf16[1536,768]{1,0:T(8,128)(2,1)} %all-gather.2.cloned.1.call-done) | copy-start | bytes 7077892
  168.7 32.4 %all-to-all-start.3 = ((f32[512,1,21]{2,1,0:T(1,128)}), f32[512,1,21]{2,1,0:T(1,128)S(1)}, u32[]{:S(2)}, u32[]{:S(2)}) async-start(f32[512,1,21]{2,1,0:T(1,128)} %broadcast_in_dim.109), calls=%async_computation.3 | async-start | bytes 524288 | tf_op jit(solution)/shard_map/all_to_all | solution.py:37
Sparse Core Ops, SparseCore 0:
  30.0 76.8 all-gather.1

commit v7 on v3

--- a/solution.py
+++ b/solution.py
@@ -13,17 +13,31 @@
 
 
 def gather_over_fsdp(w):
-    n_y = lax.axis_size("y")
+    n_y, n_z = lax.axis_size("y"), lax.axis_size("z")
     copies = jnp.broadcast_to(w[None], (n_y,) + w.shape).reshape(n_y * w.shape[0], w.shape[1])
     w = lax.all_to_all(copies, "y", 0, 0, tiled=True)
-    w = lax.all_gather(w, "xl", axis=0, tiled=True)
-    return lax.all_gather(w, "z", axis=0, tiled=True)
+    mine = lax.all_gather(w, "z", axis=0, tiled=True).reshape(n_z, 1, -1, w.shape[1])
+    return mine
+
+
+def swap_rows(mine):
+    other = lax.ppermute(mine, "xl", [(0, 1), (1, 0)])
+    first = lax.axis_index("xl") == 0
+    joined = jnp.where(
+        first, jnp.concatenate([mine, other], axis=1), jnp.concatenate([other, mine], axis=1)
+    )
+    return joined.reshape(-1, mine.shape[-1])
+
+
+def fetch_half(w):
+    width = w.shape[1] // 2
+    core = lax.axis_index("c")
+    return gather_over_fsdp(lax.dynamic_slice_in_dim(w, core * width, width, axis=1))
 
 
 def gather_weight(w):
-    width = w.shape[1] // 2
     core = lax.axis_index("c")
-    mine = gather_over_fsdp(lax.dynamic_slice_in_dim(w, core * width, width, axis=1))
+    mine = swap_rows(w)
     other = lax.ppermute(mine, "c", [(0, 1), (1, 0)])
     return jnp.where(
         core == 0, jnp.concatenate([mine, other], axis=1), jnp.concatenate([other, mine], axis=1)
@@ -96,8 +110,9 @@
     moved = lax.all_to_all(
         jnp.concatenate([outgoing, parked], axis=1), FSDP, split_axis=0, concat_axis=0, tiled=True
     )
+    half_weight, moved = lax.optimization_barrier((fetch_half(point_weight), moved))
     arrived, returned = moved[:, :out_count], moved[:, out_count:]
-    full_weight = gather_weight(point_weight)
+    full_weight = gather_weight(half_weight)
     output = jnp.dot(
         arrived[owner_slot], full_weight, preferred_element_type=jnp.float32
     ).astype(jnp.bfloat16)

time: 207 us -> 237 us (1.14)
  waiting for transfers between devices: 60.2 us -> 85.3 us
  starting transfers between devices: 55.2 us -> 61 us
  blocking collectives: 12.5 us -> 7.73 us
  other arithmetic: 29.4 us -> 31.8 us
    all_to_all x1, waiting for transfers between devices: 0.01 us -> 39.5 us  [per_device(): lax.all_to_all(jnp.concatenate([outgoing, parked], axis=1), FSDP, split_a...]
    all_gather x1, waiting for transfers between devices: 48.1 us -> 13.6 us  [gather_over_fsdp(): lax.all_gather(w, 'z', axis=0, tiled=True).reshape(n_z, 1, -1, w.shape[1])]
    ppermute x0 -> x1, waiting for transfers between devices: none -> 23.9 us  [swap_rows(): other = lax.ppermute(mine, 'xl', [(0, 1), (1, 0)])]
    all_gather x1 -> x0, blocking collectives: 4.76 us -> none  [gather_over_fsdp(): w = lax.all_gather(w, 'xl', axis=0, tiled=True)]
    all_to_all x1, waiting for transfers between devices: 3.85 us -> 0.01 us  [gather_over_fsdp(): w = lax.all_to_all(copies, 'y', 0, 0, tiled=True)]
    select_n x0 -> x1, other arithmetic: none -> 3.42 us  [swap_rows(): jnp.where(first, jnp.concatenate([mine, other], axis=1), jnp.concatenate(...]
    all_to_all x1, starting transfers between devices: 15.2 us -> 18.3 us  [per_device(): lax.all_to_all(jnp.concatenate([outgoing, parked], axis=1), FSDP, split_a...]
  transfers between devices with their start and end apart: 6 -> 7, of which waited for: 3 -> 4; matrix products, arithmetic and copies ran while one was open for 19% -> 16% of each run, Pallas kernels for 0% -> 0%
where the time goes in v7:
time: 237 us; the launch traced here: 235 us
  waiting for transfers between devices  85.3 us (36%)
  starting transfers between devices  61 us (26%)
  other arithmetic  31.8 us (13%)
  local copies, waits for them, and re-layouts  21.6 us (9%)
  between operations  14.4 us (6%)
  matrix products  13.2 us (6%)
  blocking collectives  7.73 us (3%)
    all_to_all x1, waiting for transfers between devices, per_device(): lax.all_to_all(jnp.concatenate([outgoing, parked], axis=1), FSDP, split_a...  39.5 us
    ppermute x1, waiting for transfers between devices, swap_rows(): other = lax.ppermute(mine, 'xl', [(0, 1), (1, 0)])  23.9 us
    all_to_all x1, starting transfers between devices, per_device(): lax.all_to_all(jnp.concatenate([outgoing, parked], axis=1), FSDP, split_a...  18.3 us
    all_to_all x1, starting transfers between devices, sum_all(): lax.all_to_all(jnp.broadcast_to(mine, flat.shape), FSDP, 0, 0, tiled=True)  14.3 us
    all_gather x1, waiting for transfers between devices, gather_over_fsdp(): lax.all_gather(w, 'z', axis=0, tiled=True).reshape(n_z, 1, -1, w.shape[1])  13.6 us
    all_to_all x1, starting transfers between devices, sum_all(): mine = lax.all_to_all(flat, FSDP, 0, 0, tiled=True).sum(0, keepdims=True)  12.3 us
    all_to_all x1, waiting for transfers between devices, sum_all(): lax.all_to_all(jnp.broadcast_to(mine, flat.shape), FSDP, 0, 0, tiled=True)  8.3 us
    psum x2, blocking collectives, sum_all(): mine = lax.psum(lax.psum(mine, 'c'), 'xh')  7.73 us
  transfers between devices with their start and end apart: 7, of which 4 were waited for; matrix products, arithmetic and copies ran while one was open for 16% of the time, Pallas kernels for 0%

profile of v7, /device:TPU:1, one launch (start us, length us, event | category | flops | bytes accessed | tf_op | source)
XLA Modules:
  0.0 235.1 jit_solution(12627352032825368195)
XLA Ops:
  8.7 7.6 %all-to-all-start = ((bf16[8,12,768]{2,1,0:T(8,128)(2,1)}), bf16[8,12,768]{2,1,0:T(8,128)(2,1)S(1)}, u32[]{:S(2)}, u32[]{:S(2)}) async-start(bf16[8,12,768]{2,1,0:T(8,128)(2,1)} %broadcast_in_dim.101), calls=%async_computation | async-start | bytes 393216 | tf_op jit(solution)/shard_map/all_to_all | solution.py:18
  19.7 1.8 convert_element_type.24
  26.5 2.8 %scatter_custom_fusion = bf16[256,1536]{1,0:T(8,128)(2,1)} fusion(s32[160]{0:T(256)S(1)} %bitcast.20, bf16[160,1536]{1,0:T(8,128)(2,1)} %param.17, bf16[]{:T(256)} %constant.54.clone.1), kind=kCustom, calls=%fused_computation.55 | custom fusion | bytes 786944 | tf_op jit(solution)/shard_map/scatter | solution.py:109
  29.2 2.1 gather_fusion
  34.4 18.3 %all-to-all-start.1 = ((bf16[128,2,3072]{2,1,0:T(2,128)(2,1)}), bf16[128,2,3072]{2,1,0:T(2,128)(2,1)S(1)}, u32[]{:S(2)}, u32[]{:S(2)}) async-start(bf16[128,2,3072]{2,1,0:T(2,128)(2,1)} %all_to_all.26), calls=%async_computation.1 | async-start | bytes 3145728 | tf_op jit(solution)/shard_map/all_to_all | solution.py:110
  53.5 39.5 %all-to-all-done.1 = bf16[128,2,3072]{2,1,0:T(2,128)(2,1)S(1)} async-done(((bf16[128,2,3072]{2,1,0:T(2,128)(2,1)}), bf16[128,2,3072]{2,1,0:T(2,128)(2,1)S(1)}, u32[]{:S(2)}, u32[]{:S(2)}) %all-to-all-start.1) | async-done | bytes 1572896 | tf_op jit(solution)/shard_map/all_to_all | solution.py:110
  94.4 13.6 %all-gather.2.cloned.1.call-done = bf16[768,768]{1,0:T(8,128)(2,1)} async-done(((bf16[96,768]{1,0:T(8,128)(2,1)}), bf16[768,768]{1,0:T(8,128)(2,1)}) %all-gather.2.cloned.1.call-update) | async-done | bytes 1179664 | tf_op jit(solution)/shard_map/all_gather | solution.py:19
  108.0 2.2 collective-permute-start
  110.3 23.9 %collective-permute-done = bf16[8,1,96,768]{3,2,1,0:T(8,128)(2,1)S(1)} collective-permute-done((bf16[8,1,96,768]{3,2,1,0:T(8,128)(2,1)}, bf16[8,1,96,768]{3,2,1,0:T(8,128)(2,1)S(1)}, u32[]{:S(2)}, u32[]{:S(2)}) %collective-permute-start) | collective-permute-done | bytes 1179680 | tf_op jit(solution)/shard_map/ppermute | solution.py:24
  134.2 3.4 %maximum_select_fusion.1 = bf16[8,2,96,768]{3,2,1,0:T(8,128)(2,1)} fusion(bf16[8,1,96,768]{3,2,1,0:T(8,128)(2,1)S(1)} %collective-permute-done, bf16[8,1,96,768]{3,2,1,0:T(8,128)(2,1)} %bitcast.19, pred[]{:T(512)S(6)} %eq.24), kind=kLoop, calls=%fused_computation.12 | loop fusion | flops 3538944 | bytes 4718593 | tf_op jit(solution)/shard_map/jit(_where)/select_n | solution.py:26
  137.6 6.2 %collective-permute-start.1 = (bf16[1536,768]{1,0:T(8,128)(2,1)}, bf16[1536,768]{1,0:T(8,128)(2,1)}, u32[]{:S(2)}, u32[]{:S(2)}) collective-permute-start(bf16[1536,768]{1,0:T(8,128)(2,1)} %bitcast.11), channel_id=1, source_target_pairs={{0,1},{1,0},{2,3},{3,2},{4,5},{5,4},{6,7},{7,6},{8,9},{9,8},{10,11... | collective-permute-start | bytes 7077896 | tf_op jit(solution)/shard_map/ppermute | solution.py:41
  145.0 2.8 %scatter_custom_fusion.1 = bf16[257,1536]{1,0:T(8,128)(2,1)S(1)} fusion(s32[256]{0:T(256)S(1)} %bitcast.23, bf16[256,3072]{1,0:T(8,128)(2,1)} %all_to_all.28, bf16[]{:T(256)} %constant.54.clone.1), kind=kCustom, calls=%fused_computation.51 | custom fusion | bytes 1576448 | tf_op jit(solution)/shard_map/scatter | solution.py:120
  147.8 1.8 gather_fusion.1
  149.6 6.7 %multiply_reduce_fusion = (f32[1536]{0:T(1024)S(1)}, f32[256]{0:T(256)S(1)}, f32[256]{0:T(256)S(1)}, f32[1536]{0:T(1024)S(1)}, f32[256,1536]{1,0:T(8,128)S(1)}) fusion(f32[256,1536]{1,0:T(8,128)S(1)} %get-tuple-element.26, f32[256]{0:T(256)S(1)} %fusion.19, f32[256]{0:T(256)S(1)} %broadcast_multiply_fusion.1, f32[1536]{0:T(1024)S(1)} %copy-done.6, ...), kind=kOutput, calls=%fused_computation.26 | convolution fusion | flops 1238626816 | bytes 8684033 | tf_op jit(solution)/shard_map/dot_general | solution.py:122
  157.7 2.4 %multiply_reduce_fusion.5 = (f32[1536]{0:T(1024)S(1)}, f32[1536]{0:T(1024)S(1)}, f32[1536]{0:T(1024)S(1)}, f32[1536]{0:T(1024)S(1)}, f32[1536]{0:T(1024)S(1)}, /*index=5*/f32[256,1536]{1,0:T(8,128)S(1)}) fusion(f32[256,1536]{1,0:T(8,128)S(1)} %copy-done.4, pred[256]{0:T(512)(128)(4,1)S(1)} %get-tuple-element.35, pred[256]{0:T(512)(128)(4,1)S(1)} %get-tuple-element.32, ...), kind=kLoop, calls=%fused_computation.31 | loop fusion | flops 7856640 | bytes 6333440 | tf_op jit(solution)/shard_map/transpose(jvp())/reduce_sum | solution.py:74
  160.2 3.9 %multiply_select_fusion.3 = (f32[256,1536]{1,0:T(8,128)}, f32[256,1536]{1,0:T(8,128)}, f32[256,1536]{1,0:T(8,128)}, f32[256,1536]{1,0:T(8,128)}, f32[256,1536]{1,0:T(8,128)}) fusion(f32[256,1536]{1,0:T(8,128)S(1)} %get-tuple-element.22, f32[1536]{0:T(1024)S(1)} %get-tuple-element.20, pred[256]{0:T(512)(128)(4,1)S(1)} %get-tuple-element.35, ...), kind=kLoop, calls=%fused_computation.35 | loop fusion | flops 3538944 | bytes 9468928 | tf_op jit(solution)/shard_map/transpose(jvp(jit(_where)))/select_n | solution.py:74
  164.9 12.3 %all-to-all-start.2 = ((f32[128,1,84]{2,1,0:T(1,128)}), f32[128,1,84]{2,1,0:T(1,128)S(1)}, u32[]{:S(2)}, u32[]{:S(2)}) async-start(f32[128,1,84]{2,1,0:T(1,128)} %bitcast.12), calls=%async_computation.2 | async-start | bytes 131072 | tf_op jit(solution)/shard_map/all_to_all | solution.py:50
  177.2 5.9 %fusion.4 = (f32[256,1536]{1,0:T(8,128)}, f32[256,1536]{1,0:T(8,128)S(1)}) fusion(f32[256,3072]{1,0:T(8,128)S(1)} %copy-done.2, f32[256,1536]{1,0:T(8,128)} %get-tuple-element.28, f32[256,1536]{1,0:T(8,128)} %get-tuple-element.29, f32[256,1536]{1,0:T(8,128)} %get-tuple-element.30, f32[256,1536]{1,0:T(8,128)} %get-tuple-element.31, ...), kind=kLoop, calls=%fused_computation.15 | loop fusion | flops 4718592 | bytes 14156032 | tf_op jit(solution)/shard_map/transpose(jvp())/mul | solution.py:61
  183.1 6.5 %convolution_convert_fusion.1 = bf16[160,1536]{1,0:T(8,128)(2,1)} fusion(bf16[160,1536]{1,0:T(8,128)(2,1)S(1)} %copy-done.5, bf16[1536,768]{1,0:T(8,128)(2,1)} %collective-permute-done.1, bf16[1536,768]{1,0:T(8,128)(2,1)} %bitcast.11, pred[]{:T(512)S(6)} %eq.23), kind=kOutput, calls=%fused_computation.9 | convolution fusion | flops 776454144 | bytes 5701633 | tf_op jit(solution)/shard_map/dot_general | solution.py:116
  191.3 2.5 %psum.16 = f32[1,84]{1,0:T(1,128)S(1)} all-reduce(f32[1,84]{1,0:T(1,128)S(1)} %bitcast.24), channel_id=1, replica_groups=mesh['z'=8,'xl'=2,'y'=8,'xh'=2,'c'=2] {'c'}, use_global_device_ids=true, to_apply=%region_17.18 | all-reduce | flops 84 | bytes 672 | tf_op jit(solution)/shard_map/psum | solution.py:51
  193.8 5.3 %psum.18 = f32[84]{0:T(128)S(1)} all-reduce(f32[84]{0:T(128)S(1)} %bitcast.27), channel_id=1, replica_groups=mesh['z'=8,'xl'=2,'y'=8,'xh'=2,'c'=2] {'xh'}, use_global_device_ids=true, to_apply=%region_18.19 | all-reduce | flops 84 | bytes 672 | tf_op jit(solution)/shard_map/psum | solution.py:51
  199.7 14.3 %all-to-all-start.3 = ((f32[128,1,84]{2,1,0:T(1,128)}), f32[128,1,84]{2,1,0:T(1,128)S(1)}, u32[]{:S(2)}, u32[]{:S(2)}) async-start(f32[128,1,84]{2,1,0:T(1,128)} %broadcast_in_dim.112), calls=%async_computation.3 | async-start | bytes 131072 | tf_op jit(solution)/shard_map/all_to_all | solution.py:52
  214.1 3.2 %add_convert_fusion = bf16[256,3072]{1,0:T(8,128)(2,1)} fusion(f32[256,1536]{1,0:T(8,128)} %fusion.22, f32[256,1536]{1,0:T(8,128)} %get-tuple-element.23), kind=kLoop, calls=%fused_computation.5 | loop fusion | flops 1572864 | bytes 4718592 | tf_op jit(solution)/shard_map/transpose(jvp())/convert_element_type | solution.py:60
  217.3 8.3 %all-to-all-done.3 = f32[128,1,84]{2,1,0:T(1,128)S(1)} async-done(((f32[128,1,84]{2,1,0:T(1,128)}), f32[128,1,84]{2,1,0:T(1,128)S(1)}, u32[]{:S(2)}, u32[]{:S(2)}) %all-to-all-start.3) | async-done | bytes 43040 | tf_op jit(solution)/shard_map/all_to_all | solution.py:52
  (68 shorter events, 23.5 us)
Async XLA Ops:
  7.2 0.8 copy-start
  8.7 25.8 %all-to-all-start = ((bf16[8,12,768]{2,1,0:T(8,128)(2,1)}), bf16[8,12,768]{2,1,0:T(8,128)(2,1)S(1)}, u32[]{:S(2)}, u32[]{:S(2)}) async-start(bf16[8,12,768]{2,1,0:T(8,128)(2,1)} %broadcast_in_dim.101), calls=%async_computation | async-start | bytes 393216 | tf_op jit(solution)/shard_map/all_to_all | solution.py:18
  21.4 1.7 copy-start.1
  23.1 1.7 copy-start.3
  24.8 0.7 copy-start.8
  24.8 0.7 copy-start.6
  24.8 0.7 copy-start.7
  34.4 58.5 %all-to-all-start.1 = ((bf16[128,2,3072]{2,1,0:T(2,128)(2,1)}), bf16[128,2,3072]{2,1,0:T(2,128)(2,1)S(1)}, u32[]{:S(2)}, u32[]{:S(2)}) async-start(bf16[128,2,3072]{2,1,0:T(2,128)(2,1)} %all_to_all.26), calls=%async_computation.1 | async-start | bytes 3145728 | tf_op jit(solution)/shard_map/all_to_all | solution.py:110
  52.7 55.3 %all-gather.2.cloned.1.call-start = ((), (), s32[]{:S(2)}) async-start(), calls=%async_computation.4 | async-start | bytes 1327104 | tf_op jit(solution)/shard_map/all_gather | solution.py:19
  108.0 26.2 %collective-permute-start = (bf16[8,1,96,768]{3,2,1,0:T(8,128)(2,1)}, bf16[8,1,96,768]{3,2,1,0:T(8,128)(2,1)S(1)}, u32[]{:S(2)}, u32[]{:S(2)}) collective-permute-start(bf16[8,1,96,768]{3,2,1,0:T(8,128)(2,1)} %bitcast.18), channel_id=1, source_target_pairs={{0,32},{32,0},{1,33},{33,1},{2,34},{34,2},{3,35},{35,3},{4,36},{36... | collective-permute-start | bytes 3538952 | tf_op jit(solution)/shard_map/ppermute | solution.py:24
  137.6 12.0 %collective-permute-start.1 = (bf16[1536,768]{1,0:T(8,128)(2,1)}, bf16[1536,768]{1,0:T(8,128)(2,1)}, u32[]{:S(2)}, u32[]{:S(2)}) collective-permute-start(bf16[1536,768]{1,0:T(8,128)(2,1)} %bitcast.11), channel_id=1, source_target_pairs={{0,1},{1,0},{2,3},{3,2},{4,5},{5,4},{6,7},{7,6},{8,9},{9,8},{10,11... | collective-permute-start | bytes 7077896 | tf_op jit(solution)/shard_map/ppermute | solution.py:41
  156.3 1.4 copy-start.4
  160.1 17.1 %copy-start.2 = (f32[256,3072]{1,0:T(8,128)S(1)}, f32[256,3072]{1,0:T(8,128)}, u32[]{:S(2)}) copy-start(f32[256,3072]{1,0:T(8,128)} %copy-done.1) | copy-start | bytes 9437188
  164.9 26.3 %all-to-all-start.2 = ((f32[128,1,84]{2,1,0:T(1,128)}), f32[128,1,84]{2,1,0:T(1,128)S(1)}, u32[]{:S(2)}, u32[]{:S(2)}) async-start(f32[128,1,84]{2,1,0:T(1,128)} %bitcast.12), calls=%async_computation.2 | async-start | bytes 131072 | tf_op jit(solution)/shard_map/all_to_all | solution.py:50
  177.2 5.9 %copy-start.5 = (bf16[160,1536]{1,0:T(8,128)(2,1)S(1)}, bf16[160,1536]{1,0:T(8,128)(2,1)}, u32[]{:S(2)}) copy-start(bf16[160,1536]{1,0:T(8,128)(2,1)} %gather_fusion.1) | copy-start | bytes 1474564
  199.7 25.9 %all-to-all-start.3 = ((f32[128,1,84]{2,1,0:T(1,128)}), f32[128,1,84]{2,1,0:T(1,128)S(1)}, u32[]{:S(2)}, u32[]{:S(2)}) async-start(f32[128,1,84]{2,1,0:T(1,128)} %broadcast_in_dim.112), calls=%async_computation.3 | async-start | bytes 131072 | tf_op jit(solution)/shard_map/all_to_all | solution.py:52
Sparse Core Ops, SparseCore 0:
  56.2 51.8 all-gather.1

commit v8 on v3

--- a/solution.py
+++ b/solution.py
@@ -34,7 +34,7 @@
     n_f = lax.axis_size(FSDP)
     flat = parts.reshape(n_f, -1)
     mine = lax.all_to_all(flat, FSDP, 0, 0, tiled=True).sum(0, keepdims=True)
-    mine = lax.psum(lax.psum(mine, "c"), "xh")
+    mine = lax.psum(mine, DP)
     whole = lax.all_to_all(jnp.broadcast_to(mine, flat.shape), FSDP, 0, 0, tiled=True)
     return whole.reshape(parts.shape)
 

time: 207 us -> 206 us (level)
    psum x2 -> x1, blocking collectives: 7.73 us -> 6.81 us  [sum_all(): mine = lax.psum(mine, DP)]
where the time goes in v8:
time: 206 us; the launch traced here: 204 us
  waiting for transfers between devices  60.2 us (29%)
  starting transfers between devices  55.2 us (27%)
  other arithmetic  29.4 us (14%)
  local copies, waits for them, and re-layouts  20.5 us (10%)
  between operations  14.4 us (7%)
  matrix products  12.2 us (6%)
  blocking collectives  11.6 us (6%)
    all_gather x1, waiting for transfers between devices, gather_over_fsdp(): return lax.all_gather(w, 'z', axis=0, tiled=True)  48.1 us
    all_to_all x1, starting transfers between devices, per_device(): lax.all_to_all(jnp.concatenate([outgoing, parked], axis=1), FSDP, split_a...  15.2 us
    all_to_all x1, starting transfers between devices, sum_all(): lax.all_to_all(jnp.broadcast_to(mine, flat.shape), FSDP, 0, 0, tiled=True)  14.4 us
    all_to_all x1, starting transfers between devices, sum_all(): mine = lax.all_to_all(flat, FSDP, 0, 0, tiled=True).sum(0, keepdims=True)  11.9 us
    all_to_all x1, waiting for transfers between devices, sum_all(): lax.all_to_all(jnp.broadcast_to(mine, flat.shape), FSDP, 0, 0, tiled=True)  8.3 us
    all_to_all x1, starting transfers between devices, gather_over_fsdp(): w = lax.all_to_all(copies, 'y', 0, 0, tiled=True)  7.64 us
    mul x2, other arithmetic, conv_module(): mixed_vals = values[:, :chan_count] * jax.nn.sigmoid(values[:, chan_count:])  7.53 us
    psum x1, blocking collectives, sum_all(): mine = lax.psum(mine, DP)  6.81 us
  transfers between devices with their start and end apart: 6, of which 3 were waited for; matrix products, arithmetic and copies ran while one was open for 19% of the time, Pallas kernels for 0%

profile of v8, /device:TPU:1, one launch (start us, length us, event | category | flops | bytes accessed | tf_op | source)
XLA Modules:
  0.0 203.6 jit_solution(11870533594236862968)
XLA Ops:
  8.7 7.6 %all-to-all-start.1 = ((bf16[8,12,768]{2,1,0:T(8,128)(2,1)}), bf16[8,12,768]{2,1,0:T(8,128)(2,1)S(1)}, u32[]{:S(2)}, u32[]{:S(2)}) async-start(bf16[8,12,768]{2,1,0:T(8,128)(2,1)} %broadcast_in_dim.108), calls=%async_computation.1 | async-start | bytes 393216 | tf_op jit(solution)/shard_map/all_to_all | solution.py:18
  17.2 1.8 convert_element_type.24
  21.2 3.9 %all-to-all-done.1 = bf16[8,12,768]{2,1,0:T(8,128)(2,1)S(1)} async-done(((bf16[8,12,768]{2,1,0:T(8,128)(2,1)}), bf16[8,12,768]{2,1,0:T(8,128)(2,1)S(1)}, u32[]{:S(2)}, u32[]{:S(2)}) %all-to-all-start.1) | async-done | bytes 147488 | tf_op jit(solution)/shard_map/all_to_all | solution.py:18
  25.1 4.8 %all_gather.6 = bf16[192,768]{1,0:T(8,128)(2,1)} all-gather(bf16[96,768]{1,0:T(8,128)(2,1)S(1)} %all_to_all.28), channel_id=1, replica_groups=mesh['z'=8,'xl'=2,'y'=8,'xh'=2,'c'=2] {'xl'}, dimensions={0}, use_global_device_ids=true | all-gather | bytes 442368 | tf_op jit(solution)/shard_map/all_gather | solution.py:19
  32.2 1.7 fusion.24
  35.6 2.8 %scatter_custom_fusion = bf16[256,1536]{1,0:T(8,128)(2,1)} fusion(s32[160]{0:T(256)S(1)} %bitcast.13, bf16[160,1536]{1,0:T(8,128)(2,1)} %param.17, bf16[]{:T(256)} %constant.48.clone.1), kind=kCustom, calls=%fused_computation.54 | custom fusion | bytes 786944 | tf_op jit(solution)/shard_map/scatter | solution.py:95
  38.4 2.2 %gather_fusion = bf16[256,1536]{1,0:T(8,128)(2,1)} fusion(bf16[257,1536]{1,0:T(8,128)(2,1)S(1)} %concatenate.15, s32[1024]{0:T(1024)S(1)} %pad_clamp_fusion.1), kind=kCustom, calls=%fused_computation | custom fusion | bytes 1573888 | tf_op jit(solution)/shard_map/gather | solution.py:92
  40.6 1.5 pad_maximum_fusion
  43.6 15.2 %all-to-all-start = ((bf16[128,2,3072]{2,1,0:T(2,128)(2,1)}), bf16[128,2,3072]{2,1,0:T(2,128)(2,1)S(1)}, u32[]{:S(2)}, u32[]{:S(2)}) async-start(bf16[128,2,3072]{2,1,0:T(2,128)(2,1)} %all_to_all.24), calls=%async_computation | async-start | bytes 3145728 | tf_op jit(solution)/shard_map/all_to_all | solution.py:96
  58.9 48.1 %all-gather.2.cloned.1.call-done = bf16[1536,768]{1,0:T(8,128)(2,1)} async-done(((bf16[192,768]{1,0:T(8,128)(2,1)}), bf16[1536,768]{1,0:T(8,128)(2,1)}) %all-gather.2.cloned.1.call-update) | async-done | bytes 2359312 | tf_op jit(solution)/shard_map/all_gather | solution.py:20
  106.9 6.0 %collective-permute-start = (bf16[1536,768]{1,0:T(8,128)(2,1)}, bf16[1536,768]{1,0:T(8,128)(2,1)}, u32[]{:S(2)}, u32[]{:S(2)}) collective-permute-start(bf16[1536,768]{1,0:T(8,128)(2,1)} %all-gather.2.cloned.1.call-done), channel_id=1, source_target_pairs={{0,1},{1,0},{2,3},{3,2},{4,5},{5,4},{6,7},{7,6},{8,9},{9,8},{10,11... | collective-permute-start | bytes 7077896 | tf_op jit(solution)/shard_map/ppermute | solution.py:27
  115.7 2.8 %scatter_custom_fusion.1 = bf16[257,1536]{1,0:T(8,128)(2,1)S(1)} fusion(s32[256]{0:T(256)S(1)} %bitcast.12, bf16[256,3072]{1,0:T(8,128)(2,1)} %all_to_all.26, bf16[]{:T(256)} %constant.48.clone.1), kind=kCustom, calls=%fused_computation.50 | custom fusion | bytes 1576448 | tf_op jit(solution)/shard_map/scatter | solution.py:105
  118.5 1.8 gather_fusion.1
  120.2 6.7 %multiply_reduce_fusion = (f32[1536]{0:T(1024)S(1)}, f32[256]{0:T(256)S(1)}, f32[256]{0:T(256)S(1)}, f32[1536]{0:T(1024)S(1)}, f32[256,1536]{1,0:T(8,128)S(1)}) fusion(f32[256,1536]{1,0:T(8,128)S(1)} %get-tuple-element.22, f32[256]{0:T(256)S(1)} %fusion.19, f32[256]{0:T(256)S(1)} %broadcast_multiply_fusion.1, f32[1536]{0:T(1024)S(1)} %copy-done.9, ...), kind=kOutput, calls=%fused_computation.25 | convolution fusion | flops 1238626816 | bytes 8684033 | tf_op jit(solution)/shard_map/dot_general | solution.py:107
  128.4 2.4 %multiply_reduce_fusion.5 = (f32[1536]{0:T(1024)S(1)}, f32[1536]{0:T(1024)S(1)}, f32[1536]{0:T(1024)S(1)}, f32[1536]{0:T(1024)S(1)}, f32[1536]{0:T(1024)S(1)}, /*index=5*/f32[256,1536]{1,0:T(8,128)S(1)}) fusion(f32[256,1536]{1,0:T(8,128)S(1)} %copy-done.4, pred[256]{0:T(512)(128)(4,1)S(1)} %get-tuple-element.31, pred[256]{0:T(512)(128)(4,1)S(1)} %get-tuple-element.28, ...), kind=kLoop, calls=%fused_computation.30 | loop fusion | flops 7856640 | bytes 6333440 | tf_op jit(solution)/shard_map/transpose(jvp())/reduce_sum | solution.py:60
  130.8 3.9 %multiply_select_fusion.3 = (f32[256,1536]{1,0:T(8,128)}, f32[256,1536]{1,0:T(8,128)}, f32[256,1536]{1,0:T(8,128)}, f32[256,1536]{1,0:T(8,128)}, f32[256,1536]{1,0:T(8,128)}) fusion(f32[256,1536]{1,0:T(8,128)S(1)} %get-tuple-element.18, f32[1536]{0:T(1024)S(1)} %copy-done.7, pred[256]{0:T(512)(128)(4,1)S(1)} %get-tuple-element.31, ...), kind=kLoop, calls=%fused_computation.34 | loop fusion | flops 3538944 | bytes 9468928 | tf_op jit(solution)/shard_map/transpose(jvp(jit(_where)))/select_n | solution.py:60
  135.6 11.9 %all-to-all-start.2 = ((f32[128,1,84]{2,1,0:T(1,128)}), f32[128,1,84]{2,1,0:T(1,128)S(1)}, u32[]{:S(2)}, u32[]{:S(2)}) async-start(f32[128,1,84]{2,1,0:T(1,128)} %bitcast.7), calls=%async_computation.2 | async-start | bytes 131072 | tf_op jit(solution)/shard_map/all_to_all | solution.py:36
  147.5 6.0 %fusion.4 = (f32[256,1536]{1,0:T(8,128)}, f32[256,1536]{1,0:T(8,128)S(1)}) fusion(f32[256,3072]{1,0:T(8,128)S(1)} %copy-done.2, f32[256,1536]{1,0:T(8,128)} %get-tuple-element.24, f32[256,1536]{1,0:T(8,128)} %get-tuple-element.25, f32[256,1536]{1,0:T(8,128)} %get-tuple-element.26, f32[256,1536]{1,0:T(8,128)} %get-tuple-element.27, ...), kind=kLoop, calls=%fused_computation.14 | loop fusion | flops 4718592 | bytes 14156032 | tf_op jit(solution)/shard_map/transpose(jvp())/mul | solution.py:47
  153.5 5.4 %convolution_convert_fusion.1 = bf16[160,1536]{1,0:T(8,128)(2,1)} fusion(bf16[160,1536]{1,0:T(8,128)(2,1)S(1)} %copy-done.5, bf16[1536,768]{1,0:T(8,128)(2,1)} %collective-permute-done, bf16[1536,768]{1,0:T(8,128)(2,1)S(1)} %copy-done.14, pred[]{:T(512)S(6)} %eq.20), kind=kOutput, calls=%fused_computation.9 | convolution fusion | flops 776454144 | bytes 5701633 | tf_op jit(solution)/shard_map/dot_general | solution.py:101
  158.9 1.6 fusion.22
  160.7 6.8 %psum.10 = f32[84]{0:T(128)S(1)} all-reduce(f32[84]{0:T(128)S(1)} %reduce_sum.146), channel_id=1, replica_groups=mesh['z'=8,'xl'=2,'y'=8,'xh'=2,'c'=2] {'xh','c'}, use_global_device_ids=true, to_apply=%region_17.18 | all-reduce | flops 84 | bytes 672 | tf_op jit(solution)/shard_map/psum | solution.py:37
  168.1 14.4 %all-to-all-start.3 = ((f32[128,1,84]{2,1,0:T(1,128)}), f32[128,1,84]{2,1,0:T(1,128)S(1)}, u32[]{:S(2)}, u32[]{:S(2)}) async-start(f32[128,1,84]{2,1,0:T(1,128)} %broadcast_in_dim.112), calls=%async_computation.3 | async-start | bytes 131072 | tf_op jit(solution)/shard_map/all_to_all | solution.py:38
  182.5 3.2 %add_convert_fusion = bf16[256,3072]{1,0:T(8,128)(2,1)} fusion(f32[256,1536]{1,0:T(8,128)} %fusion.22, f32[256,1536]{1,0:T(8,128)} %get-tuple-element.19), kind=kLoop, calls=%fused_computation.5 | loop fusion | flops 1572864 | bytes 4718592 | tf_op jit(solution)/shard_map/transpose(jvp())/convert_element_type | solution.py:46
  185.7 8.3 %all-to-all-done.3 = f32[128,1,84]{2,1,0:T(1,128)S(1)} async-done(((f32[128,1,84]{2,1,0:T(1,128)}), f32[128,1,84]{2,1,0:T(1,128)S(1)}, u32[]{:S(2)}, u32[]{:S(2)}) %all-to-all-start.3) | async-done | bytes 43040 | tf_op jit(solution)/shard_map/all_to_all | solution.py:38
  (77 shorter events, 18.5 us)
Async XLA Ops:
  7.2 0.8 copy-start
  8.7 16.4 %all-to-all-start.1 = ((bf16[8,12,768]{2,1,0:T(8,128)(2,1)}), bf16[8,12,768]{2,1,0:T(8,128)(2,1)S(1)}, u32[]{:S(2)}, u32[]{:S(2)}) async-start(bf16[8,12,768]{2,1,0:T(8,128)(2,1)} %broadcast_in_dim.108), calls=%async_computation.1 | async-start | bytes 393216 | tf_op jit(solution)/shard_map/all_to_all | solution.py:18
  16.3 90.6 %all-gather.2.cloned.1.call-start = ((), (), s32[]{:S(2)}) async-start(), calls=%async_computation.4 | async-start | bytes 2654208 | tf_op jit(solution)/shard_map/all_gather | solution.py:20
  17.2 3.3 %copy-start.10 = (f32[5,1536]{1,0:T(8,128)S(1)}, f32[5,1536]{1,0:T(8,128)}, u32[]{:S(2)}) copy-start(f32[5,1536]{1,0:T(8,128)} %param.13) | copy-start | bytes 92164
  19.0 13.0 %copy-start.1 = (f32[256,3072]{1,0:T(8,128)}, f32[256,3072]{1,0:T(8,128)S(1)}, u32[]{:S(2)}) copy-start(f32[256,3072]{1,0:T(8,128)S(1)} %convert_element_type.24) | copy-start | bytes 9437188
  31.5 0.7 copy-start.6
  31.5 0.7 copy-start.7
  31.5 0.7 copy-start.8
  31.9 2.0 copy-start.3
  33.9 0.7 copy-start.9
  33.9 0.7 copy-start.11
  34.6 1.0 copy-start.12
  35.5 2.9 %copy-start.13 = (s32[1,256]{1,0:T(1,128)S(1)}, s32[1,256]{1,0:T(1,128)}, u32[]{:S(2)}) copy-start(s32[1,256]{1,0:T(1,128)} %param.11) | copy-start | bytes 3076
  43.6 69.3 %all-to-all-start = ((bf16[128,2,3072]{2,1,0:T(2,128)(2,1)}), bf16[128,2,3072]{2,1,0:T(2,128)(2,1)S(1)}, u32[]{:S(2)}, u32[]{:S(2)}) async-start(bf16[128,2,3072]{2,1,0:T(2,128)(2,1)} %all_to_all.24), calls=%async_computation | async-start | bytes 3145728 | tf_op jit(solution)/shard_map/all_to_all | solution.py:96
  106.9 13.3 %collective-permute-start = (bf16[1536,768]{1,0:T(8,128)(2,1)}, bf16[1536,768]{1,0:T(8,128)(2,1)}, u32[]{:S(2)}, u32[]{:S(2)}) collective-permute-start(bf16[1536,768]{1,0:T(8,128)(2,1)} %all-gather.2.cloned.1.call-done), channel_id=1, source_target_pairs={{0,1},{1,0},{2,3},{3,2},{4,5},{5,4},{6,7},{7,6},{8,9},{9,8},{10,11... | collective-permute-start | bytes 7077896 | tf_op jit(solution)/shard_map/ppermute | solution.py:27
  127.0 1.4 copy-start.4
  130.8 16.7 %copy-start.2 = (f32[256,3072]{1,0:T(8,128)S(1)}, f32[256,3072]{1,0:T(8,128)}, u32[]{:S(2)}) copy-start(f32[256,3072]{1,0:T(8,128)} %copy-done.1) | copy-start | bytes 9437188
  135.6 25.0 %all-to-all-start.2 = ((f32[128,1,84]{2,1,0:T(1,128)}), f32[128,1,84]{2,1,0:T(1,128)S(1)}, u32[]{:S(2)}, u32[]{:S(2)}) async-start(f32[128,1,84]{2,1,0:T(1,128)} %bitcast.7), calls=%async_computation.2 | async-start | bytes 131072 | tf_op jit(solution)/shard_map/all_to_all | solution.py:36
  147.5 6.0 %copy-start.5 = (bf16[160,1536]{1,0:T(8,128)(2,1)S(1)}, bf16[160,1536]{1,0:T(8,128)(2,1)}, u32[]{:S(2)}) copy-start(bf16[160,1536]{1,0:T(8,128)(2,1)} %gather_fusion.1) | copy-start | bytes 1474564
  147.5 6.0 %copy-start.14 = (bf16[1536,768]{1,0:T(8,128)(2,1)S(1)}, bf16[1536,768]{1,0:T(8,128)(2,1)}, u32[]{:S(2)}) copy-start(bf16[1536,768]{1,0:T(8,128)(2,1)} %all-gather.2.cloned.1.call-done) | copy-start | bytes 7077892
  168.1 25.9 %all-to-all-start.3 = ((f32[128,1,84]{2,1,0:T(1,128)}), f32[128,1,84]{2,1,0:T(1,128)S(1)}, u32[]{:S(2)}, u32[]{:S(2)}) async-start(f32[128,1,84]{2,1,0:T(1,128)} %broadcast_in_dim.112), calls=%async_computation.3 | async-start | bytes 131072 | tf_op jit(solution)/shard_map/all_to_all | solution.py:38
Sparse Core Ops, SparseCore 0:
  30.0 76.8 all-gather.1
